TPU v7x, 512 devices: a whole 4x8x8 slice. The times are simulated.
512 devices in a mesh: dp: 16 (over z, core), mp: 32 (over x, y).
Axes of the slice: x: 4, y: 8, z: 8, core: 2. Of those that a mesh axis runs over, the one named last changes fastest.
Arguments:
- tokens: bfloat16 [2048, 4096], P(('dp', 'mp')), may hold values from -6 to 6
- hidden_grad: bfloat16 [2048, 14336], P('dp', 'mp'), may hold values from -0.125 to 0.125
- gate_weight: bfloat16 [4096, 14336], P('dp', 'mp'), may hold values from -0.09375 to 0.09375
- up_weight: bfloat16 [4096, 14336], P('dp', 'mp'), may hold values from -0.09375 to 0.09375
- gate_probe: bfloat16 [4096, 14336], P('dp', 'mp'), may hold values from -1 to 1, as said below
- gate_mean: float32 [4096, 14336], P('dp', 'mp'), may hold values from -0.6 to 0.6
- gate_curve: float32 [4096, 14336], P('dp', 'mp'), may hold values from 1 to 10
- group_counts: int32 [16], replicated, may hold values from 32 to 128, as said below
Outputs:
- gate_weight_new: bfloat16 [4096, 14336], P('dp', 'mp')
- gate_mean_new: float32 [4096, 14336], P('dp', 'mp')
- gate_curve_new: float32 [4096, 14336], P('dp', 'mp')
Inputs may be any that keep to these rules, and one draw needn't show every extreme that they name: `group_counts`: some data group has exactly 128 live tokens in every draw. `gate_probe`: every entry is -1 or 1, each sign drawn independently.
All inputs are finite; a program needn't handle non-finite values.
Results may differ from a plain program's by a relative error of at most 0.0017.
Values may be sent and summed in bfloat16 or wider, within the bound.
No kernel may reach another device: no remote copies, remote signals or barrier semaphores. Data moves between devices by JAX's collectives and lax.ppermute only.
A program may use at most 64 MiB of HBM per device.

v0:
```python
import jax
import jax.numpy as jnp
from jax import lax
from jax.sharding import PartitionSpec as P

first_decay = 0.9
second_decay = 0.999
learn_rate = 0.15
epsilon_term = 0.0001
first_fix = 1.0 - 0.9**10
second_fix = 1.0 - 0.999**10


def silu_parts(inputs):
    sigmoid_part = jax.nn.sigmoid(inputs)
    silu_slope = sigmoid_part * (1.0 + inputs * (1.0 - sigmoid_part))
    silu_bend = sigmoid_part * (1.0 - sigmoid_part) * (2.0 + inputs * (1.0 - 2.0 * sigmoid_part))
    return (silu_slope, silu_bend)


def adahessian(weight, mean_old, curve_old, gradient, probe_value, product):
    diagonal = probe_value.astype(jnp.float32) * product
    mean_new = first_decay * mean_old + (1.0 - first_decay) * gradient
    curve_new = second_decay * curve_old + (1.0 - second_decay) * diagonal * diagonal
    step_ratio = mean_new / first_fix / (jnp.sqrt(curve_new / second_fix) + epsilon_term)
    weight_new = (weight.astype(jnp.float32) - learn_rate * step_ratio).astype(jnp.bfloat16)
    return (weight_new, mean_new, curve_new)


def body(
    tokens, hidden_grad, gate_weight, up_weight, gate_probe, gate_mean, gate_curve, group_counts
):
    whole = lax.all_gather(tokens, "mp", axis=0, tiled=True)
    columns = lax.all_to_all(whole, "dp", split_axis=1, concat_axis=0, tiled=True)
    group_rows = whole.shape[0]
    width = gate_weight.shape[1]
    pieces = (
        lax.all_gather(gate_weight, "dp", axis=0, tiled=True),
        lax.all_gather(up_weight, "dp", axis=0, tiled=True),
    )
    gate_pre, up_pre = tuple(
        (jnp.dot(whole, piece, preferred_element_type=jnp.float32) for piece in pieces)
    )
    selected = columns
    gate_tan = lax.psum_scatter(
        jnp.dot(selected, gate_probe, preferred_element_type=jnp.float32),
        "dp",
        scatter_dimension=0,
        tiled=True,
    )
    group_index = lax.axis_index("dp")
    limit = lax.dynamic_index_in_dim(group_counts, group_index, 0, keepdims=False)
    live = (jnp.arange(group_rows, dtype=jnp.int32) < limit).astype(jnp.float32)
    silu_slope, silu_bend = silu_parts(gate_pre)
    masked = hidden_grad.astype(jnp.float32) * live[:, None]
    grad_gate = (masked * up_pre * silu_slope).astype(jnp.bfloat16)
    tan_gate = (masked * up_pre * silu_bend * gate_tan).astype(jnp.bfloat16)
    packed = jnp.concatenate([grad_gate, tan_gate], 1)
    selected = columns
    sums = lax.dot_general(
        selected,
        lax.all_gather(packed, "dp", axis=0, tiled=True),
        (((0,), (0,)), ((), ())),
        preferred_element_type=jnp.float32,
    )
    gate_out = adahessian(
        gate_weight, gate_mean, gate_curve, sums[:, :width], gate_probe, sums[:, width:]
    )
    return (gate_out[0], gate_out[1], gate_out[2])


def solution(mesh):
    return jax.shard_map(
        body,
        mesh=mesh,
        in_specs=(
            P(("dp", "mp"), None),
            P("dp", "mp"),
            P("dp", "mp"),
            P("dp", "mp"),
            P("dp", "mp"),
            P("dp", "mp"),
            P("dp", "mp"),
            P(),
        ),
        out_specs=(P("dp", "mp"), P("dp", "mp"), P("dp", "mp")),
        check_vma=False,
    )
```

profile of v0, /device:TPU:1, one launch (start us, length us, event | category | flops | bytes accessed | tf_op | source)
XLA Modules:
  0.0 342.0 jit_solution(2087898380235495970)
XLA Ops:
  7.2 0.0 copy-start.2
  7.2 0.0 all-gather.12.cloned.1.call-start
  7.2 0.7 all-gather.12.cloned.1.call-update
  7.9 0.0 all-gather.8.cloned.1.call-start
  8.0 0.7 all-gather.8.cloned.1.call-update
  8.7 0.0 all-gather.6.cloned.1.call-start
  8.7 0.7 all-gather.6.cloned.1.call-update
  9.4 0.0 reduce-scatter.2.cloned.1.call-start
  9.4 83.9 %all-gather.12.cloned.1.call-done = bf16[32,4,4096]{2,1,0:T(4,128)(2,1)} async-done(((bf16[1,4,4096]{2,1,0:T(4,128)(2,1)}), bf16[32,4,4096]{2,1,0:T(4,128)(2,1)}) %all-gather.12.cloned.1.call-update) | async-done | bytes 1048592 | tf_op jit(solution)/shard_map/all_gather | solution.py:33
  93.3 1.8 all_to_all.14
  95.1 0.3 copy.12
  95.5 47.8 %all_to_all.19 = bf16[128,16,256]{2,0,1:T(8,128)(2,1)S(1)} all-to-all(bf16[128,16,256]{2,0,1:T(8,128)(2,1)S(1)} %copy.12), channel_id=1, replica_groups=mesh['dp'=16,'mp'=32] {'dp'}, dimensions={1} | all-to-all | bytes 2097152 | tf_op jit(solution)/shard_map/all_to_all | solution.py:34
  143.3 0.0 copy-done.2
  143.3 2.6 fusion.13
  145.9 0.0 copy-start.6
  145.9 0.0 copy-start
  145.9 0.0 reduce-scatter.2.cloned.1.call-update
  145.9 0.0 copy-start.5
  145.9 0.0 all-gather.10.cloned.1.call-start
  146.0 0.6 copy-done.6
  146.5 0.6 dynamic_slice.4
  147.1 0.6 compare_convert_fusion
  147.8 0.0 copy-done
  147.8 0.3 reshape.15
  148.1 15.2 %all-gather.8.cloned.1.call-done = bf16[4096,448]{0,1:T(8,128)(2,1)} async-done(((bf16[256,448]{0,1:T(8,128)(2,1)}), bf16[4096,448]{0,1:T(8,128)(2,1)}) %all-gather.8.cloned.1.call-update) | async-done | bytes 3670032 | tf_op jit(solution)/shard_map/all_gather | solution.py:38
  163.3 3.1 fusion.12
  166.5 45.4 %all-gather.6.cloned.1.call-done = bf16[4096,448]{0,1:T(8,128)(2,1)} async-done(((bf16[256,448]{0,1:T(8,128)(2,1)}), bf16[4096,448]{0,1:T(8,128)(2,1)}) %all-gather.6.cloned.1.call-update) | async-done | bytes 3670032 | tf_op jit(solution)/shard_map/all_gather | solution.py:39
  211.9 63.9 %reduce-scatter.2.cloned.1.call-done = f32[128,448]{0,1:T(8,128)} async-done(((f32[2048,448]{0,1:T(8,128)}), f32[128,448]{0,1:T(8,128)}) %reduce-scatter.2.cloned.1.call-update) | async-done | bytes 229392 | tf_op jit(solution)/shard_map/reduce_scatter | solution.py:45
  275.8 0.0 copy-done.5
  275.8 3.2 fusion.5
  278.9 0.7 pad_maximum_fusion
  279.6 0.0 all-gather.10.cloned.1.call-update
  279.7 0.0 copy-start.1
  279.7 0.0 copy-start.3
  279.7 0.0 copy-start.4
  279.7 51.3 %all-gather.10.cloned.1.call-done = bf16[2048,896]{0,1:T(8,128)(2,1)} async-done(((bf16[128,896]{0,1:T(8,128)(2,1)}), bf16[2048,896]{0,1:T(8,128)(2,1)}) %all-gather.10.cloned.1.call-update) | async-done | bytes 3670032 | tf_op jit(solution)/shard_map/all_gather | solution.py:62
  331.0 3.1 convolution_bitcast_fusion
  334.2 0.0 copy-done.1
  334.2 0.0 copy-done.3
  334.2 0.0 copy-done.4
  334.2 1.2 subtract_convert_fusion
Async XLA Ops:
  7.2 136.1 %copy-start.2 = (bf16[256,448]{0,1:T(8,128)(2,1)S(1)}, bf16[256,448]{0,1:T(8,128)(2,1)}, u32[]{:S(2)}) copy-start(bf16[256,448]{0,1:T(8,128)(2,1)} %param.12) | copy-start | bytes 688132
  7.2 86.2 %all-gather.12.cloned.1.call-start = ((), (), s32[]{:S(2)}) async-start(), calls=%async_computation.6 | async-start | bytes 1081344 | tf_op jit(solution)/shard_map/all_gather | solution.py:33
  7.9 155.4 %all-gather.8.cloned.1.call-start = ((), (), s32[]{:S(2)}) async-start(), calls=%async_computation.3 | async-start | bytes 3899392 | tf_op jit(solution)/shard_map/all_gather | solution.py:38
  8.7 203.2 %all-gather.6.cloned.1.call-start = ((), (), s32[]{:S(2)}) async-start(), calls=%async_computation.2 | async-start | bytes 3899392 | tf_op jit(solution)/shard_map/all_gather | solution.py:39
  9.4 266.4 %reduce-scatter.2.cloned.1.call-start = ((), (), s32[]{:S(2)}) async-start(), calls=%async_computation.4 | async-start | bytes 3899392 | tf_op jit(solution)/shard_map/reduce_scatter | solution.py:45
  145.9 0.7 copy-start.6
  145.9 1.9 copy-start
  145.9 129.9 %copy-start.5 = (bf16[128,448]{0,1:T(8,128)(2,1)S(1)}, bf16[128,448]{0,1:T(8,128)(2,1)}, u32[]{:S(2)}) copy-start(bf16[128,448]{0,1:T(8,128)(2,1)} %param.9) | copy-start | bytes 344068
  145.9 185.1 %all-gather.10.cloned.1.call-start = ((), (), s32[]{:S(2)}) async-start(), calls=%async_computation.5 | async-start | bytes 3899392 | tf_op jit(solution)/shard_map/all_gather | solution.py:62
  279.7 54.5 %copy-start.1 = (bf16[256,448]{0,1:T(8,128)(2,1)S(1)}, bf16[256,448]{0,1:T(8,128)(2,1)}, u32[]{:S(2)}) copy-start(bf16[256,448]{0,1:T(8,128)(2,1)} %param.10) | copy-start | bytes 688132
  279.7 54.5 %copy-start.3 = (f32[256,448]{0,1:T(8,128)S(1)}, f32[256,448]{0,1:T(8,128)}, u32[]{:S(2)}) copy-start(f32[256,448]{0,1:T(8,128)} %param.13) | copy-start | bytes 1376260
  279.7 54.5 %copy-start.4 = (f32[256,448]{0,1:T(8,128)S(1)}, f32[256,448]{0,1:T(8,128)}, u32[]{:S(2)}) copy-start(f32[256,448]{0,1:T(8,128)} %param.14) | copy-start | bytes 1376260
Sparse Core Ops, SparseCore 0:
  11.2 82.1 all-gather.11
  95.4 67.8 all-gather.7
  165.4 46.4 all-gather.5
  214.6 61.1 reduce-scatter.1
  279.8 51.2 all-gather.9
where the time goes:
time: 342 us
  waiting for transfers between devices  262 us (77%)
  blocking collectives  47.8 us (14%)
  between operations  13.9 us (4%)
  matrix products  12 us (4%)
  local copies, waits for them, and re-layouts  3.58 us (1%)
    all_gather x1, waiting for transfers between devices, body(): whole = lax.all_gather(tokens, 'mp', axis=0, tiled=True)  83.9 us
    reduce_scatter x1, waiting for transfers between devices, body(): lax.psum_scatter(jnp.dot(selected, gate_probe, preferred_element_type=jnp...  63.9 us
    all_gather x1, waiting for transfers between devices, body(): lax.all_gather(packed, 'dp', axis=0, tiled=True)  51.3 us
    all_to_all x1, blocking collectives, body(): lax.all_to_all(whole, 'dp', split_axis=1, concat_axis=0, tiled=True)  47.8 us
    all_gather x1, waiting for transfers between devices, body(): lax.all_gather(up_weight, 'dp', axis=0, tiled=True)  45.4 us
    all_gather x1, waiting for transfers between devices, body(): lax.all_gather(gate_weight, 'dp', axis=0, tiled=True)  15.2 us
  transfers between devices with their start and end apart: 5, of which 5 were waited for; matrix products, arithmetic and copies ran while one was open for 2% of the time, Pallas kernels for 0%

commit v1 on v0

--- a/solution.py
+++ b/solution.py
@@ -27,42 +27,83 @@
     return (weight_new, mean_new, curve_new)
 
 
+def chip_ring(x, n_dp):
+    n_chip = n_dp // 2
+    d = lax.axis_index("dp")
+    z = d // 2
+    c = d % 2
+    rows = x.shape[0]
+    partner = [(i, i ^ 1) for i in range(n_dp)]
+    ring = [(2 * j, 2 * ((j + 1) % n_chip)) for j in range(n_chip)] + [
+        (2 * j + 1, 2 * ((j - 1) % n_chip) + 1) for j in range(n_chip)
+    ]
+    px = lax.ppermute(x, "dp", partner)
+    pieces = [(x, d), (px, d ^ 1)]
+    cur = jnp.concatenate([x, px], 0)
+    step = 2 * c - 1
+    for k in range(1, n_chip // 2 + 1):
+        cur = lax.ppermute(cur, "dp", ring)
+        j = (z + k * step) % n_chip
+        o = c
+        pieces.append((cur[:rows], 2 * j + o))
+        pieces.append((cur[rows:], 2 * j + 1 - o))
+        if k < n_chip // 2:
+            ex = lax.ppermute(cur, "dp", partner)
+            j2 = (z - k * step) % n_chip
+            o2 = 1 - c
+            pieces.append((ex[:rows], 2 * j2 + o2))
+            pieces.append((ex[rows:], 2 * j2 + 1 - o2))
+    return pieces
+
+
 def body(
     tokens, hidden_grad, gate_weight, up_weight, gate_probe, gate_mean, gate_curve, group_counts
 ):
-    whole = lax.all_gather(tokens, "mp", axis=0, tiled=True)
-    columns = lax.all_to_all(whole, "dp", split_axis=1, concat_axis=0, tiled=True)
+    n_dp = lax.axis_size("dp")
+    n_mp = lax.axis_size("mp")
+    rows_loc, feat = tokens.shape
+    shard = feat // n_dp
+    width = gate_weight.shape[1]
+    d = lax.axis_index("dp")
+
+    t3 = tokens.reshape(rows_loc, n_dp, shard)
+    a2a = lax.all_to_all(t3, "dp", split_axis=1, concat_axis=1, tiled=True)
+    pack = jnp.concatenate([tokens, a2a.reshape(rows_loc, feat)], 0)
+    gathered = lax.all_gather(pack, "mp", axis=0, tiled=False)
+    whole = gathered[:, :rows_loc, :].reshape(n_mp * rows_loc, feat)
     group_rows = whole.shape[0]
-    width = gate_weight.shape[1]
-    pieces = (
-        lax.all_gather(gate_weight, "dp", axis=0, tiled=True),
-        lax.all_gather(up_weight, "dp", axis=0, tiled=True),
+    cols = (
+        gathered[:, rows_loc:, :]
+        .reshape(n_mp, rows_loc, n_dp, shard)
+        .transpose(2, 0, 1, 3)
+        .reshape(n_dp * group_rows, shard)
     )
-    gate_pre, up_pre = tuple(
-        (jnp.dot(whole, piece, preferred_element_type=jnp.float32) for piece in pieces)
-    )
-    selected = columns
-    gate_tan = lax.psum_scatter(
-        jnp.dot(selected, gate_probe, preferred_element_type=jnp.float32),
-        "dp",
-        scatter_dimension=0,
-        tiled=True,
-    )
-    group_index = lax.axis_index("dp")
-    limit = lax.dynamic_index_in_dim(group_counts, group_index, 0, keepdims=False)
+
+    w3 = jnp.concatenate([gate_weight, up_weight, gate_probe], 1)
+    pre = None
+    for piece, s in chip_ring(w3, n_dp):
+        part = lax.dynamic_slice_in_dim(whole, s * shard, shard, axis=1)
+        term = jnp.dot(part, piece, preferred_element_type=jnp.float32)
+        pre = term if pre is None else pre + term
+    gate_pre = pre[:, :width]
+    up_pre = pre[:, width : 2 * width]
+    gate_tan = pre[:, 2 * width :]
+
+    limit = lax.dynamic_index_in_dim(group_counts, d, 0, keepdims=False)
     live = (jnp.arange(group_rows, dtype=jnp.int32) < limit).astype(jnp.float32)
     silu_slope, silu_bend = silu_parts(gate_pre)
     masked = hidden_grad.astype(jnp.float32) * live[:, None]
     grad_gate = (masked * up_pre * silu_slope).astype(jnp.bfloat16)
     tan_gate = (masked * up_pre * silu_bend * gate_tan).astype(jnp.bfloat16)
     packed = jnp.concatenate([grad_gate, tan_gate], 1)
-    selected = columns
-    sums = lax.dot_general(
-        selected,
-        lax.all_gather(packed, "dp", axis=0, tiled=True),
-        (((0,), (0,)), ((), ())),
-        preferred_element_type=jnp.float32,
-    )
+
+    sums = None
+    for piece, g in chip_ring(packed, n_dp):
+        part = lax.dynamic_slice_in_dim(cols, g * group_rows, group_rows, axis=0)
+        term = lax.dot_general(
+            part, piece, (((0,), (0,)), ((), ())), preferred_element_type=jnp.float32
+        )
+        sums = term if sums is None else sums + term
     gate_out = adahessian(
         gate_weight, gate_mean, gate_curve, sums[:, :width], gate_probe, sums[:, width:]
     )

time: 342 us -> 214 us (0.63)
  waiting for transfers between devices: 262 us -> 73 us
  starting transfers between devices: 0.19 us -> 59.2 us
  blocking collectives: 47.8 us -> 19.2 us
  local copies, waits for them, and re-layouts: 3.58 us -> 17.7 us
  matrix products: 12 us -> 24.9 us
    all_gather x4 -> x1, waiting for transfers between devices: 196 us -> 20.3 us  [body(): gathered = lax.all_gather(pack, 'mp', axis=0, tiled=False)]
    reduce_scatter x1 -> x0, waiting for transfers between devices: 63.9 us -> none  [body(): lax.psum_scatter(jnp.dot(selected, gate_probe, preferred_element_type=jnp...]
    ppermute x0 -> x16, starting transfers between devices: none -> 59.2 us  [the longest x6 26.2 us: chip_ring(): ex = lax.ppermute(cur, 'dp', partner)]
    ppermute x0 -> x16, waiting for transfers between devices: none -> 52.7 us  [the longest x8 49.8 us: chip_ring(): cur = lax.ppermute(cur, 'dp', ring)]
    all_to_all x1, blocking collectives: 47.8 us -> 19.2 us  [body(): a2a = lax.all_to_all(t3, 'dp', split_axis=1, concat_axis=1, tiled=True)]
    dot_general x4 -> x32, matrix products: 12 us -> 24.9 us  [the longest x16 17.7 us: body(): term = jnp.dot(part, piece, preferred_element_type=jnp.float32)]
    unnamed x15 -> x39, local copies, waits for them, and re-layouts: 0.88 us -> 10.9 us
  transfers between devices with their start and end apart: 5 -> 17, of which waited for: 5 -> 9; matrix products, arithmetic and copies ran while one was open for 2% -> 17% of each run, Pallas kernels for 0% -> 0%
where the time goes in v1:
time: 214 us; the launch traced here: 213 us
  waiting for transfers between devices  73 us (34%)
  starting transfers between devices  59.2 us (28%)
  matrix products  24.9 us (12%)
  blocking collectives  19.2 us (9%)
  local copies, waits for them, and re-layouts  17.7 us (8%)
  between operations  15 us (7%)
  other arithmetic  3.74 us (2%)
    ppermute x8, waiting for transfers between devices, chip_ring(): cur = lax.ppermute(cur, 'dp', ring)  49.8 us
    ppermute x6, starting transfers between devices, chip_ring(): ex = lax.ppermute(cur, 'dp', partner)  26.2 us
    ppermute x8, starting transfers between devices, chip_ring(): cur = lax.ppermute(cur, 'dp', ring)  22.5 us
    all_gather x1, waiting for transfers between devices, body(): gathered = lax.all_gather(pack, 'mp', axis=0, tiled=False)  20.3 us
    all_to_all x1, blocking collectives, body(): a2a = lax.all_to_all(t3, 'dp', split_axis=1, concat_axis=1, tiled=True)  19.2 us
    dot_general x16, matrix products, body(): term = jnp.dot(part, piece, preferred_element_type=jnp.float32)  17.7 us
    unnamed x39, local copies, waits for them, and re-layouts  10.9 us
    ppermute x2, starting transfers between devices, chip_ring(): px = lax.ppermute(x, 'dp', partner)  10.4 us
  transfers between devices with their start and end apart: 17, of which 9 were waited for; matrix products, arithmetic and copies ran while one was open for 17% of the time, Pallas kernels for 0%

profile of v1, /device:TPU:1, one launch (start us, length us, event | category | flops | bytes accessed | tf_op | source)
XLA Modules:
  0.0 212.8 jit_solution(12686609841888425118)
XLA Ops:
  7.2 19.2 %all_to_all.5 = bf16[4,16,256]{2,0,1:T(4,128)(2,1)S(1)} all-to-all(bf16[4,16,256]{2,0,1:T(4,128)(2,1)} %bitcast.11), channel_id=1, replica_groups=mesh['dp'=16,'mp'=32] {'dp'}, dimensions={1} | all-to-all | bytes 65536 | tf_op jit(solution)/shard_map/all_to_all | solution.py:70
  26.4 1.4 pad_maximum_fusion.3
  27.9 1.0 constant_dynamic-update-slice_fusion.2
  28.8 1.0 constant_dynamic-update-slice_fusion.1
  29.8 1.0 constant_dynamic-update-slice_fusion
  30.8 2.4 %collective-permute-start = (bf16[256,1344]{0,1:T(8,128)(2,1)S(1)}, bf16[256,1344]{0,1:T(8,128)(2,1)S(1)}, u32[]{:S(2)}, u32[]{:S(2)}) collective-permute-start(bf16[256,1344]{0,1:T(8,128)(2,1)S(1)} %constant_dynamic-update-slice_fusion), channel_id=1, source_target_pairs={{0,32},{32,0},{64,96},{96,64},{128,160},{160,128},{192,224},{224,1... | collective-permute-start | bytes 2064392 | tf_op jit(solution)/shard_map/ppermute | solution.py:40
  33.2 1.7 collective-permute-done
  35.1 0.7 copy-done.1
  35.8 2.1 %collective-permute-start.1 = (bf16[512,1344]{0,1:T(8,128)(2,1)S(1)}, bf16[512,1344]{0,1:T(8,128)(2,1)}, u32[]{:S(2)}, u32[]{:S(2)}) collective-permute-start(bf16[512,1344]{0,1:T(8,128)(2,1)S(1)} %pad_maximum_fusion), channel_id=1, source_target_pairs={{0,64},{64,128},{128,192},{192,256},{256,320},{320,384},{384,448},... | collective-permute-start | bytes 4128776 | tf_op jit(solution)/shard_map/ppermute | solution.py:45
  38.0 17.3 %collective-permute-done.1 = bf16[512,1344]{0,1:T(8,128)(2,1)} collective-permute-done((bf16[512,1344]{0,1:T(8,128)(2,1)S(1)}, bf16[512,1344]{0,1:T(8,128)(2,1)}, u32[]{:S(2)}, u32[]{:S(2)}) %collective-permute-start.1) | collective-permute-done | bytes 1376288 | tf_op jit(solution)/shard_map/ppermute | solution.py:45
  55.3 3.1 %collective-permute-start.3 = (bf16[512,1344]{0,1:T(8,128)(2,1)}, bf16[512,1344]{0,1:T(8,128)(2,1)}, u32[]{:S(2)}, u32[]{:S(2)}) collective-permute-start(bf16[512,1344]{0,1:T(8,128)(2,1)} %collective-permute-done.1), channel_id=1, source_target_pairs={{0,64},{64,128},{128,192},{192,256},{256,320},{320,384},{384,448},... | collective-permute-start | bytes 4128776 | tf_op jit(solution)/shard_map/ppermute | solution.py:45
  58.6 0.6 dynamic_slice.101
  59.2 0.6 compare_convert_fusion
  59.8 3.2 %collective-permute-start.2 = (bf16[512,1344]{0,1:T(8,128)(2,1)}, bf16[512,1344]{0,1:T(8,128)(2,1)}, u32[]{:S(2)}, u32[]{:S(2)}) collective-permute-start(bf16[512,1344]{0,1:T(8,128)(2,1)} %collective-permute-done.1), channel_id=1, source_target_pairs={{0,32},{32,0},{64,96},{96,64},{128,160},{160,128},{192,224},{224,1... | collective-permute-start | bytes 4128776 | tf_op jit(solution)/shard_map/ppermute | solution.py:51
  63.1 11.9 %collective-permute-done.3 = bf16[512,1344]{0,1:T(8,128)(2,1)} collective-permute-done((bf16[512,1344]{0,1:T(8,128)(2,1)}, bf16[512,1344]{0,1:T(8,128)(2,1)}, u32[]{:S(2)}, u32[]{:S(2)}) %collective-permute-start.3) | collective-permute-done | bytes 1376288 | tf_op jit(solution)/shard_map/ppermute | solution.py:45
  74.9 6.4 %collective-permute-start.4 = (bf16[512,1344]{0,1:T(8,128)(2,1)}, bf16[512,1344]{0,1:T(8,128)(2,1)}, u32[]{:S(2)}, u32[]{:S(2)}) collective-permute-start(bf16[512,1344]{0,1:T(8,128)(2,1)} %collective-permute-done.3), channel_id=1, source_target_pairs={{0,32},{32,0},{64,96},{96,64},{128,160},{160,128},{192,224},{224,1... | collective-permute-start | bytes 4128776 | tf_op jit(solution)/shard_map/ppermute | solution.py:51
  81.3 1.9 collective-permute-start.5
  83.3 20.3 %all-gather.3.cloned.1.call-done = bf16[256,4096]{1,0:T(8,128)(2,1)} async-done(((bf16[8,4096]{1,0:T(8,128)(2,1)}), bf16[256,4096]{1,0:T(8,128)(2,1)}) %all-gather.3.cloned.1.call-update) | async-done | bytes 2097168 | tf_op jit(solution)/shard_map/all_gather | solution.py:72
  103.6 3.4 %fusion.146 = (bf16[32,4,4096]{2,1,0:T(4,128)(2,1)S(1)}, bf16[32,4,4096]{2,1,0:T(4,128)(2,1)S(1)}) fusion(bf16[32,8,4096]{2,1,0:T(8,128)(2,1)} %bitcast.10), kind=kLoop, calls=%fused_computation.170 | loop fusion | bytes 4194304 | tf_op jit(solution)/shard_map/slice | solution.py:76
  107.2 1.4 fusion.108
  108.7 1.4 fusion.41
  110.1 1.5 fusion.36
  111.7 1.4 fusion.34
  113.5 1.4 fusion.38
  114.9 1.5 fusion
  116.4 5.3 %collective-permute-start.7 = (bf16[512,1344]{0,1:T(8,128)(2,1)}, bf16[512,1344]{0,1:T(8,128)(2,1)S(1)}, u32[]{:S(2)}, u32[]{:S(2)}) collective-permute-start(bf16[512,1344]{0,1:T(8,128)(2,1)} %collective-permute-done.5), channel_id=1, source_target_pairs={{0,64},{64,128},{128,192},{192,256},{256,320},{320,384},{384,448},... | collective-permute-start | bytes 4128776 | tf_op jit(solution)/shard_map/ppermute | solution.py:45
  121.8 1.5 fusion.3
  123.2 4.6 %collective-permute-start.6 = (bf16[512,1344]{0,1:T(8,128)(2,1)}, bf16[512,1344]{0,1:T(8,128)(2,1)S(1)}, u32[]{:S(2)}, u32[]{:S(2)}) collective-permute-start(bf16[512,1344]{0,1:T(8,128)(2,1)} %collective-permute-done.5), channel_id=1, source_target_pairs={{0,32},{32,0},{64,96},{96,64},{128,160},{160,128},{192,224},{224,1... | collective-permute-start | bytes 4128776 | tf_op jit(solution)/shard_map/ppermute | solution.py:51
  127.8 1.4 fusion.29
  129.3 1.4 fusion.27
  130.8 1.4 fusion.31
  132.2 1.5 fusion.6
  133.7 3.6 %collective-permute-done.7 = bf16[512,1344]{0,1:T(8,128)(2,1)S(1)} collective-permute-done((bf16[512,1344]{0,1:T(8,128)(2,1)}, bf16[512,1344]{0,1:T(8,128)(2,1)S(1)}, u32[]{:S(2)}, u32[]{:S(2)}) %collective-permute-start.7) | collective-permute-done | bytes 1376288 | tf_op jit(solution)/shard_map/ppermute | solution.py:45
  138.4 0.4 fusion.9
  138.7 0.5 copy-done.13
  139.5 8.0 %collective-permute-start.8 = (bf16[128,896]{0,1:T(8,128)(2,1)S(1)}, bf16[128,896]{0,1:T(8,128)(2,1)S(1)}, u32[]{:S(2)}, u32[]{:S(2)}) collective-permute-start(bf16[128,896]{0,1:T(8,128)(2,1)S(1)} %pad_maximum_fusion.2), channel_id=1, source_target_pairs={{0,32},{32,0},{64,96},{96,64},{128,160},{160,128},{192,224},{224,1... | collective-permute-start | bytes 688136 | tf_op jit(solution)/shard_map/ppermute | solution.py:40
  147.5 1.1 collective-permute-done.8
  148.6 0.8 pad_maximum_fusion.1
  149.4 3.6 %collective-permute-start.9 = (bf16[256,896]{0,1:T(8,128)(2,1)}, bf16[256,896]{0,1:T(8,128)(2,1)}, u32[]{:S(2)}, u32[]{:S(2)}) collective-permute-start(bf16[256,896]{0,1:T(8,128)(2,1)} %pad_maximum_fusion.1), channel_id=1, source_target_pairs={{0,64},{64,128},{128,192},{192,256},{256,320},{320,384},{384,448},... | collective-permute-start | bytes 1376264 | tf_op jit(solution)/shard_map/ppermute | solution.py:45
  153.2 0.8 copy.34
  154.0 0.9 copy.39
  154.9 1.0 copy.35
  155.9 1.0 copy.38
  156.9 0.8 reshape.32
  157.7 0.5 copy.37
  159.5 4.1 %collective-permute-start.10 = (bf16[256,896]{0,1:T(8,128)(2,1)}, bf16[256,896]{0,1:T(8,128)(2,1)S(1)}, u32[]{:S(2)}, u32[]{:S(2)}) collective-permute-start(bf16[256,896]{0,1:T(8,128)(2,1)} %collective-permute-done.9), channel_id=1, source_target_pairs={{0,32},{32,0},{64,96},{96,64},{128,160},{160,128},{192,224},{224,1... | collective-permute-start | bytes 1376264 | tf_op jit(solution)/shard_map/ppermute | solution.py:51
  163.6 2.4 %collective-permute-start.11 = (bf16[256,896]{0,1:T(8,128)(2,1)}, bf16[256,896]{0,1:T(8,128)(2,1)S(1)}, u32[]{:S(2)}, u32[]{:S(2)}) collective-permute-start(bf16[256,896]{0,1:T(8,128)(2,1)} %collective-permute-done.9), channel_id=1, source_target_pairs={{0,64},{64,128},{128,192},{192,256},{256,320},{320,384},{384,448},... | collective-permute-start | bytes 1376264 | tf_op jit(solution)/shard_map/ppermute | solution.py:45
  166.0 1.3 fusion.75
  167.3 1.3 fusion.19
  168.6 4.8 %collective-permute-done.11 = bf16[256,896]{0,1:T(8,128)(2,1)S(1)} collective-permute-done((bf16[256,896]{0,1:T(8,128)(2,1)}, bf16[256,896]{0,1:T(8,128)(2,1)S(1)}, u32[]{:S(2)}, u32[]{:S(2)}) %collective-permute-start.11) | collective-permute-done | bytes 458784 | tf_op jit(solution)/shard_map/ppermute | solution.py:45
  173.3 4.0 %collective-permute-start.12 = (bf16[256,896]{0,1:T(8,128)(2,1)S(1)}, bf16[256,896]{0,1:T(8,128)(2,1)S(1)}, u32[]{:S(2)}, u32[]{:S(2)}) collective-permute-start(bf16[256,896]{0,1:T(8,128)(2,1)S(1)} %collective-permute-done.11), channel_id=1, source_target_pairs={{0,32},{32,0},{64,96},{96,64},{128,160},{160,128},{192,224},{224,1... | collective-permute-start | bytes 1376264 | tf_op jit(solution)/shard_map/ppermute | solution.py:51
  177.3 1.9 collective-permute-start.13
  180.2 0.4 fusion.18
  180.6 6.2 %collective-permute-done.13 = bf16[256,896]{0,1:T(8,128)(2,1)S(1)} collective-permute-done((bf16[256,896]{0,1:T(8,128)(2,1)S(1)}, bf16[256,896]{0,1:T(8,128)(2,1)S(1)}, u32[]{:S(2)}, u32[]{:S(2)}) %collective-permute-start.13) | collective-permute-done | bytes 458784 | tf_op jit(solution)/shard_map/ppermute | solution.py:45
  186.8 4.0 %collective-permute-start.14 = (bf16[256,896]{0,1:T(8,128)(2,1)S(1)}, bf16[256,896]{0,1:T(8,128)(2,1)S(1)}, u32[]{:S(2)}, u32[]{:S(2)}) collective-permute-start(bf16[256,896]{0,1:T(8,128)(2,1)S(1)} %collective-permute-done.13), channel_id=1, source_target_pairs={{0,32},{32,0},{64,96},{96,64},{128,160},{160,128},{192,224},{224,1... | collective-permute-start | bytes 1376264 | tf_op jit(solution)/shard_map/ppermute | solution.py:51
  190.8 2.1 collective-permute-start.15
  193.9 0.4 fusion.15
  194.3 6.0 %collective-permute-done.15 = bf16[256,896]{0,1:T(8,128)(2,1)S(1)} collective-permute-done((bf16[256,896]{0,1:T(8,128)(2,1)S(1)}, bf16[256,896]{0,1:T(8,128)(2,1)S(1)}, u32[]{:S(2)}, u32[]{:S(2)}) %collective-permute-start.15) | collective-permute-done | bytes 458784 | tf_op jit(solution)/shard_map/ppermute | solution.py:45
  201.3 0.4 fusion.12
  201.8 0.6 copy-done.3
  202.7 0.5 subtract_convert_fusion
  203.2 1.0 copy.41
  204.2 1.0 copy.42
  205.1 0.8 copy.40
  (57 shorter events, 6.5 us)
Async XLA Ops:
  7.2 96.4 %all-gather.3.cloned.1.call-start = ((), (), s32[]{:S(2)}) async-start(), calls=%async_computation.1 | async-start | bytes 2162688 | tf_op jit(solution)/shard_map/all_gather | solution.py:72
  30.8 4.3 %copy-start = (bf16[256,1344]{0,1:T(8,128)(2,1)}, bf16[256,1344]{0,1:T(8,128)(2,1)S(1)}, u32[]{:S(2)}) copy-start(bf16[256,1344]{0,1:T(8,128)(2,1)S(1)} %constant_dynamic-update-slice_fusion) | copy-start | bytes 2064388
  30.8 27.8 %copy-start.14 = (s32[16]{0:T(128)S(1)}, s32[16]{0:T(128)}, u32[]{:S(2)}) copy-start(s32[16]{0:T(128)} %param.15) | copy-start | bytes 196
  30.8 4.2 %collective-permute-start = (bf16[256,1344]{0,1:T(8,128)(2,1)S(1)}, bf16[256,1344]{0,1:T(8,128)(2,1)S(1)}, u32[]{:S(2)}, u32[]{:S(2)}) collective-permute-start(bf16[256,1344]{0,1:T(8,128)(2,1)S(1)} %constant_dynamic-update-slice_fusion), channel_id=1, source_target_pairs={{0,32},{32,0},{64,96},{96,64},{128,160},{160,128},{192,224},{224,1... | collective-permute-start | bytes 2064392 | tf_op jit(solution)/shard_map/ppermute | solution.py:40
  35.0 0.9 copy-start.1
  35.8 19.4 %collective-permute-start.1 = (bf16[512,1344]{0,1:T(8,128)(2,1)S(1)}, bf16[512,1344]{0,1:T(8,128)(2,1)}, u32[]{:S(2)}, u32[]{:S(2)}) collective-permute-start(bf16[512,1344]{0,1:T(8,128)(2,1)S(1)} %pad_maximum_fusion), channel_id=1, source_target_pairs={{0,64},{64,128},{128,192},{192,256},{256,320},{320,384},{384,448},... | collective-permute-start | bytes 4128776 | tf_op jit(solution)/shard_map/ppermute | solution.py:45
  55.3 19.7 %collective-permute-start.3 = (bf16[512,1344]{0,1:T(8,128)(2,1)}, bf16[512,1344]{0,1:T(8,128)(2,1)}, u32[]{:S(2)}, u32[]{:S(2)}) collective-permute-start(bf16[512,1344]{0,1:T(8,128)(2,1)} %collective-permute-done.1), channel_id=1, source_target_pairs={{0,64},{64,128},{128,192},{192,256},{256,320},{320,384},{384,448},... | collective-permute-start | bytes 4128776 | tf_op jit(solution)/shard_map/ppermute | solution.py:45
  59.8 53.6 %collective-permute-start.2 = (bf16[512,1344]{0,1:T(8,128)(2,1)}, bf16[512,1344]{0,1:T(8,128)(2,1)}, u32[]{:S(2)}, u32[]{:S(2)}) collective-permute-start(bf16[512,1344]{0,1:T(8,128)(2,1)} %collective-permute-done.1), channel_id=1, source_target_pairs={{0,32},{32,0},{64,96},{96,64},{128,160},{160,128},{192,224},{224,1... | collective-permute-start | bytes 4128776 | tf_op jit(solution)/shard_map/ppermute | solution.py:51
  74.9 55.8 %collective-permute-start.4 = (bf16[512,1344]{0,1:T(8,128)(2,1)}, bf16[512,1344]{0,1:T(8,128)(2,1)}, u32[]{:S(2)}, u32[]{:S(2)}) collective-permute-start(bf16[512,1344]{0,1:T(8,128)(2,1)} %collective-permute-done.3), channel_id=1, source_target_pairs={{0,32},{32,0},{64,96},{96,64},{128,160},{160,128},{192,224},{224,1... | collective-permute-start | bytes 4128776 | tf_op jit(solution)/shard_map/ppermute | solution.py:51
  81.3 35.1 %collective-permute-start.5 = (bf16[512,1344]{0,1:T(8,128)(2,1)}, bf16[512,1344]{0,1:T(8,128)(2,1)}, u32[]{:S(2)}, u32[]{:S(2)}) collective-permute-start(bf16[512,1344]{0,1:T(8,128)(2,1)} %collective-permute-done.3), channel_id=1, source_target_pairs={{0,64},{64,128},{128,192},{192,256},{256,320},{320,384},{384,448},... | collective-permute-start | bytes 4128776 | tf_op jit(solution)/shard_map/ppermute | solution.py:45
  110.1 3.0 %copy-start.2 = (bf16[256,1344]{0,1:T(8,128)(2,1)S(1)}, bf16[256,1344]{0,1:T(8,128)(2,1)}, u32[]{:S(2)}) copy-start(bf16[256,1344]{0,1:T(8,128)(2,1)} %copy-done.1) | copy-start | bytes 2064388
  116.4 20.9 %collective-permute-start.7 = (bf16[512,1344]{0,1:T(8,128)(2,1)}, bf16[512,1344]{0,1:T(8,128)(2,1)S(1)}, u32[]{:S(2)}, u32[]{:S(2)}) collective-permute-start(bf16[512,1344]{0,1:T(8,128)(2,1)} %collective-permute-done.5), channel_id=1, source_target_pairs={{0,64},{64,128},{128,192},{192,256},{256,320},{320,384},{384,448},... | collective-permute-start | bytes 4128776 | tf_op jit(solution)/shard_map/ppermute | solution.py:45
  123.2 14.8 %collective-permute-start.6 = (bf16[512,1344]{0,1:T(8,128)(2,1)}, bf16[512,1344]{0,1:T(8,128)(2,1)S(1)}, u32[]{:S(2)}, u32[]{:S(2)}) collective-permute-start(bf16[512,1344]{0,1:T(8,128)(2,1)} %collective-permute-done.5), channel_id=1, source_target_pairs={{0,32},{32,0},{64,96},{96,64},{128,160},{160,128},{192,224},{224,1... | collective-permute-start | bytes 4128776 | tf_op jit(solution)/shard_map/ppermute | solution.py:51
  138.3 0.9 copy-start.13
  139.3 13.9 %copy-start.9 = (bf16[256,448]{0,1:T(8,128)(2,1)S(1)}, bf16[256,448]{0,1:T(8,128)(2,1)}, u32[]{:S(2)}) copy-start(bf16[256,448]{0,1:T(8,128)(2,1)} %param.10) | copy-start | bytes 688132
  139.3 14.8 %copy-start.10 = (bf16[256,448]{0,1:T(8,128)(2,1)S(1)}, bf16[256,448]{0,1:T(8,128)(2,1)}, u32[]{:S(2)}) copy-start(bf16[256,448]{0,1:T(8,128)(2,1)} %param.12) | copy-start | bytes 688132
  139.4 15.5 %copy-start.11 = (f32[256,448]{0,1:T(8,128)S(1)}, f32[256,448]{0,1:T(8,128)}, u32[]{:S(2)}) copy-start(f32[256,448]{0,1:T(8,128)} %param.13) | copy-start | bytes 1376260
  139.5 16.4 %copy-start.12 = (f32[256,448]{0,1:T(8,128)S(1)}, f32[256,448]{0,1:T(8,128)}, u32[]{:S(2)}) copy-start(f32[256,448]{0,1:T(8,128)} %param.14) | copy-start | bytes 1376260
  139.5 9.1 %collective-permute-start.8 = (bf16[128,896]{0,1:T(8,128)(2,1)S(1)}, bf16[128,896]{0,1:T(8,128)(2,1)S(1)}, u32[]{:S(2)}, u32[]{:S(2)}) collective-permute-start(bf16[128,896]{0,1:T(8,128)(2,1)S(1)} %pad_maximum_fusion.2), channel_id=1, source_target_pairs={{0,32},{32,0},{64,96},{96,64},{128,160},{160,128},{192,224},{224,1... | collective-permute-start | bytes 688136 | tf_op jit(solution)/shard_map/ppermute | solution.py:40
  148.6 7.3 %copy-start.7 = (bf16[128,896]{0,1:T(8,128)(2,1)}, bf16[128,896]{0,1:T(8,128)(2,1)S(1)}, u32[]{:S(2)}) copy-start(bf16[128,896]{0,1:T(8,128)(2,1)S(1)} %collective-permute-done.8) | copy-start | bytes 688132
  149.4 10.1 %collective-permute-start.9 = (bf16[256,896]{0,1:T(8,128)(2,1)}, bf16[256,896]{0,1:T(8,128)(2,1)}, u32[]{:S(2)}, u32[]{:S(2)}) collective-permute-start(bf16[256,896]{0,1:T(8,128)(2,1)} %pad_maximum_fusion.1), channel_id=1, source_target_pairs={{0,64},{64,128},{128,192},{192,256},{256,320},{320,384},{384,448},... | collective-permute-start | bytes 1376264 | tf_op jit(solution)/shard_map/ppermute | solution.py:45
  158.2 0.9 copy-start.8
  159.5 20.4 %collective-permute-start.10 = (bf16[256,896]{0,1:T(8,128)(2,1)}, bf16[256,896]{0,1:T(8,128)(2,1)S(1)}, u32[]{:S(2)}, u32[]{:S(2)}) collective-permute-start(bf16[256,896]{0,1:T(8,128)(2,1)} %collective-permute-done.9), channel_id=1, source_target_pairs={{0,32},{32,0},{64,96},{96,64},{128,160},{160,128},{192,224},{224,1... | collective-permute-start | bytes 1376264 | tf_op jit(solution)/shard_map/ppermute | solution.py:51
  163.6 9.7 %collective-permute-start.11 = (bf16[256,896]{0,1:T(8,128)(2,1)}, bf16[256,896]{0,1:T(8,128)(2,1)S(1)}, u32[]{:S(2)}, u32[]{:S(2)}) collective-permute-start(bf16[256,896]{0,1:T(8,128)(2,1)} %collective-permute-done.9), channel_id=1, source_target_pairs={{0,64},{64,128},{128,192},{192,256},{256,320},{320,384},{384,448},... | collective-permute-start | bytes 1376264 | tf_op jit(solution)/shard_map/ppermute | solution.py:45
  173.3 20.2 %collective-permute-start.12 = (bf16[256,896]{0,1:T(8,128)(2,1)S(1)}, bf16[256,896]{0,1:T(8,128)(2,1)S(1)}, u32[]{:S(2)}, u32[]{:S(2)}) collective-permute-start(bf16[256,896]{0,1:T(8,128)(2,1)S(1)} %collective-permute-done.11), channel_id=1, source_target_pairs={{0,32},{32,0},{64,96},{96,64},{128,160},{160,128},{192,224},{224,1... | collective-permute-start | bytes 1376264 | tf_op jit(solution)/shard_map/ppermute | solution.py:51
  177.3 9.5 %collective-permute-start.13 = (bf16[256,896]{0,1:T(8,128)(2,1)S(1)}, bf16[256,896]{0,1:T(8,128)(2,1)S(1)}, u32[]{:S(2)}, u32[]{:S(2)}) collective-permute-start(bf16[256,896]{0,1:T(8,128)(2,1)S(1)} %collective-permute-done.11), channel_id=1, source_target_pairs={{0,64},{64,128},{128,192},{192,256},{256,320},{320,384},{384,448},... | collective-permute-start | bytes 1376264 | tf_op jit(solution)/shard_map/ppermute | solution.py:45
  186.8 14.2 %collective-permute-start.14 = (bf16[256,896]{0,1:T(8,128)(2,1)S(1)}, bf16[256,896]{0,1:T(8,128)(2,1)S(1)}, u32[]{:S(2)}, u32[]{:S(2)}) collective-permute-start(bf16[256,896]{0,1:T(8,128)(2,1)S(1)} %collective-permute-done.13), channel_id=1, source_target_pairs={{0,32},{32,0},{64,96},{96,64},{128,160},{160,128},{192,224},{224,1... | collective-permute-start | bytes 1376264 | tf_op jit(solution)/shard_map/ppermute | solution.py:51
  190.8 9.5 %collective-permute-start.15 = (bf16[256,896]{0,1:T(8,128)(2,1)S(1)}, bf16[256,896]{0,1:T(8,128)(2,1)S(1)}, u32[]{:S(2)}, u32[]{:S(2)}) collective-permute-start(bf16[256,896]{0,1:T(8,128)(2,1)S(1)} %collective-permute-done.13), channel_id=1, source_target_pairs={{0,64},{64,128},{128,192},{192,256},{256,320},{320,384},{384,448},... | collective-permute-start | bytes 1376264 | tf_op jit(solution)/shard_map/ppermute | solution.py:45
  201.3 1.0 copy-start.3
  201.3 1.2 copy-start.4
  201.3 1.2 copy-start.5
  201.3 1.3 copy-start.6
Sparse Core Ops, SparseCore 0:
  28.0 75.5 all-gather.2

commit v2 on v1

--- a/solution.py
+++ b/solution.py
@@ -27,9 +27,13 @@
     return (weight_new, mean_new, curve_new)
 
 
+DP = ("z", "c")
+MP = ("x", "y")
+
+
 def chip_ring(x, n_dp):
     n_chip = n_dp // 2
-    d = lax.axis_index("dp")
+    d = lax.axis_index(DP)
     z = d // 2
     c = d % 2
     rows = x.shape[0]
@@ -37,18 +41,18 @@
     ring = [(2 * j, 2 * ((j + 1) % n_chip)) for j in range(n_chip)] + [
         (2 * j + 1, 2 * ((j - 1) % n_chip) + 1) for j in range(n_chip)
     ]
-    px = lax.ppermute(x, "dp", partner)
+    px = lax.ppermute(x, DP, partner)
     pieces = [(x, d), (px, d ^ 1)]
     cur = jnp.concatenate([x, px], 0)
     step = 2 * c - 1
     for k in range(1, n_chip // 2 + 1):
-        cur = lax.ppermute(cur, "dp", ring)
+        cur = lax.ppermute(cur, DP, ring)
         j = (z + k * step) % n_chip
         o = c
         pieces.append((cur[:rows], 2 * j + o))
         pieces.append((cur[rows:], 2 * j + 1 - o))
         if k < n_chip // 2:
-            ex = lax.ppermute(cur, "dp", partner)
+            ex = lax.ppermute(cur, DP, partner)
             j2 = (z - k * step) % n_chip
             o2 = 1 - c
             pieces.append((ex[:rows], 2 * j2 + o2))
@@ -59,21 +63,23 @@
 def body(
     tokens, hidden_grad, gate_weight, up_weight, gate_probe, gate_mean, gate_curve, group_counts
 ):
-    n_dp = lax.axis_size("dp")
-    n_mp = lax.axis_size("mp")
+    n_dp = lax.axis_size(DP)
+    n_mp = lax.axis_size(MP)
     rows_loc, feat = tokens.shape
     shard = feat // n_dp
     width = gate_weight.shape[1]
-    d = lax.axis_index("dp")
+    d = lax.axis_index(DP)
 
+    def gather_mp(a):
+        a = lax.all_gather(a, "y", axis=0, tiled=True)
+        return lax.all_gather(a, "x", axis=0, tiled=True)
+
+    whole = gather_mp(tokens)
+    group_rows = whole.shape[0]
     t3 = tokens.reshape(rows_loc, n_dp, shard)
-    a2a = lax.all_to_all(t3, "dp", split_axis=1, concat_axis=1, tiled=True)
-    pack = jnp.concatenate([tokens, a2a.reshape(rows_loc, feat)], 0)
-    gathered = lax.all_gather(pack, "mp", axis=0, tiled=False)
-    whole = gathered[:, :rows_loc, :].reshape(n_mp * rows_loc, feat)
-    group_rows = whole.shape[0]
+    a2a = lax.all_to_all(t3, DP, split_axis=1, concat_axis=1, tiled=True)
     cols = (
-        gathered[:, rows_loc:, :]
+        gather_mp(a2a)
         .reshape(n_mp, rows_loc, n_dp, shard)
         .transpose(2, 0, 1, 3)
         .reshape(n_dp * group_rows, shard)
@@ -111,19 +117,25 @@
 
 
 def solution(mesh):
+    n_dp, n_mp = mesh.devices.shape
+    n_x = len({dev.coords[0] for dev in mesh.devices[0]})
+    mesh4 = jax.sharding.Mesh(
+        mesh.devices.reshape(n_dp // 2, 2, n_x, n_mp // n_x), ("z", "c", "x", "y")
+    )
+    every = DP + MP
     return jax.shard_map(
         body,
-        mesh=mesh,
+        mesh=mesh4,
         in_specs=(
-            P(("dp", "mp"), None),
-            P("dp", "mp"),
-            P("dp", "mp"),
-            P("dp", "mp"),
-            P("dp", "mp"),
-            P("dp", "mp"),
-            P("dp", "mp"),
+            P(every, None),
+            P(DP, MP),
+            P(DP, MP),
+            P(DP, MP),
+            P(DP, MP),
+            P(DP, MP),
+            P(DP, MP),
             P(),
         ),
-        out_specs=(P("dp", "mp"), P("dp", "mp"), P("dp", "mp")),
+        out_specs=(P(DP, MP), P(DP, MP), P(DP, MP)),
         check_vma=False,
     )

time: 214 us -> 221 us (1.033)
  blocking collectives: 19.2 us -> 42.5 us
  waiting for transfers between devices: 73 us -> 56.7 us
  starting transfers between devices: 59.2 us -> 70.4 us
  matrix products: 24.9 us -> 19 us
  local copies, waits for them, and re-layouts: 17.7 us -> 12.3 us
    all_gather x0 -> x2, blocking collectives: none -> 42.5 us  [gather_mp(): a = lax.all_gather(a, 'y', axis=0, tiled=True)]
    all_gather x1 -> x2, waiting for transfers between devices: 20.3 us -> 0.04 us  [gather_mp(): return lax.all_gather(a, 'x', axis=0, tiled=True)]
    all_to_all x1 -> x0, blocking collectives: 19.2 us -> none  [body(): a2a = lax.all_to_all(t3, 'dp', split_axis=1, concat_axis=1, tiled=True)]
    all_to_all x0 -> x1, waiting for transfers between devices: none -> 13.6 us  [body(): a2a = lax.all_to_all(t3, DP, split_axis=1, concat_axis=1, tiled=True)]
    ppermute x16, waiting for transfers between devices: 52.7 us -> 43 us  [the longest x8 40 us: chip_ring(): cur = lax.ppermute(cur, DP, ring)]
    all_to_all x0 -> x1, starting transfers between devices: none -> 9.46 us  [body(): a2a = lax.all_to_all(t3, DP, split_axis=1, concat_axis=1, tiled=True)]
    dot_general x16, matrix products: 17.7 us -> 10.8 us  [body(): term = jnp.dot(part, piece, preferred_element_type=jnp.float32)]
    slice x1 -> x0, local copies, waits for them, and re-layouts: 3.39 us -> none  [body(): gathered[:, rows_loc:, :].reshape(n_mp, rows_loc, n_dp, shard)]
  transfers between devices with their start and end apart: 17 -> 19, of which waited for: 9 -> 9; matrix products, arithmetic and copies ran while one was open for 17% -> 12% of each run, Pallas kernels for 0% -> 0%
where the time goes in v2:
time: 221 us; the launch traced here: 219 us
  starting transfers between devices  70.4 us (32%)
  waiting for transfers between devices  56.7 us (26%)
  blocking collectives  42.5 us (19%)
  matrix products  19 us (9%)
  between operations  15 us (7%)
  local copies, waits for them, and re-layouts  12.3 us (6%)
  other arithmetic  3.25 us (1%)
    all_gather x2, blocking collectives, gather_mp(): a = lax.all_gather(a, 'y', axis=0, tiled=True)  42.5 us
    ppermute x8, waiting for transfers between devices, chip_ring(): cur = lax.ppermute(cur, DP, ring)  40 us
    ppermute x6, starting transfers between devices, chip_ring(): ex = lax.ppermute(cur, DP, partner)  25.4 us
    ppermute x8, starting transfers between devices, chip_ring(): cur = lax.ppermute(cur, DP, ring)  20.6 us
    ppermute x2, starting transfers between devices, chip_ring(): px = lax.ppermute(x, DP, partner)  14.8 us
    all_to_all x1, waiting for transfers between devices, body(): a2a = lax.all_to_all(t3, DP, split_axis=1, concat_axis=1, tiled=True)  13.6 us
    dot_general x16, matrix products, body(): term = jnp.dot(part, piece, preferred_element_type=jnp.float32)  10.8 us
    all_to_all x1, starting transfers between devices, body(): a2a = lax.all_to_all(t3, DP, split_axis=1, concat_axis=1, tiled=True)  9.46 us
  transfers between devices with their start and end apart: 19, of which 9 were waited for; matrix products, arithmetic and copies ran while one was open for 12% of the time, Pallas kernels for 0%

profile of v2, /device:TPU:1, one launch (start us, length us, event | category | flops | bytes accessed | tf_op | source)
XLA Modules:
  0.0 219.1 jit_solution(13233006125582500672)
XLA Ops:
  7.2 1.0 constant_dynamic-update-slice_fusion.2
  8.2 1.0 constant_dynamic-update-slice_fusion.1
  9.1 1.0 constant_dynamic-update-slice_fusion
  10.1 8.7 %collective-permute-start = (bf16[256,1344]{0,1:T(8,128)(2,1)S(1)}, bf16[256,1344]{0,1:T(8,128)(2,1)S(1)}, u32[]{:S(2)}, u32[]{:S(2)}) collective-permute-start(bf16[256,1344]{0,1:T(8,128)(2,1)S(1)} %constant_dynamic-update-slice_fusion), channel_id=1, source_target_pairs={{0,32},{32,0},{64,96},{96,64},{128,160},{160,128},{192,224},{224,1... | collective-permute-start | bytes 2064392 | tf_op jit(solution)/shard_map/ppermute | solution.py:44
  18.8 1.7 collective-permute-done
  20.7 5.3 %collective-permute-start.1 = (bf16[512,1344]{0,1:T(8,128)(2,1)S(1)}, bf16[512,1344]{0,1:T(8,128)(2,1)}, u32[]{:S(2)}, u32[]{:S(2)}) collective-permute-start(bf16[512,1344]{0,1:T(8,128)(2,1)S(1)} %pad_maximum_fusion), channel_id=1, source_target_pairs={{0,64},{64,128},{128,192},{192,256},{256,320},{320,384},{384,448},... | collective-permute-start | bytes 4128776 | tf_op jit(solution)/shard_map/ppermute | solution.py:49
  26.0 22.0 %all-gather = bf16[8,4,4096]{2,1,0:T(4,128)(2,1)S(1)} all-gather(bf16[1,4,4096]{2,1,0:T(4,128)(2,1)} %bitcast.4), channel_id=1, replica_groups=mesh['z'=8,'c'=2,'x'=4,'y'=8] {'y'}, dimensions={0}, use_global_device_ids=true | all-gather | bytes 294912 | tf_op jit(solution)/shard_map/all_gather | solution.py:74
  48.1 0.8 reshape.24
  48.9 1.9 collective-permute-start.3
  50.8 9.5 %all-to-all-start = ((bf16[4,16,256]{2,0,1:T(4,128)(2,1)}), bf16[4,16,256]{2,0,1:T(4,128)(2,1)S(1)}, u32[]{:S(2)}, u32[]{:S(2)}) async-start(bf16[4,16,256]{2,0,1:T(4,128)(2,1)} %bitcast), calls=%async_computation | async-start | bytes 65536 | tf_op jit(solution)/shard_map/all_to_all | solution.py:80
  60.6 0.6 dynamic_slice.101
  61.2 0.6 compare_convert_fusion
  61.8 13.6 %all-to-all-done = bf16[4,16,256]{2,0,1:T(4,128)(2,1)S(1)} async-done(((bf16[4,16,256]{2,0,1:T(4,128)(2,1)}), bf16[4,16,256]{2,0,1:T(4,128)(2,1)S(1)}, u32[]{:S(2)}, u32[]{:S(2)}) %all-to-all-start) | async-done | bytes 32800 | tf_op jit(solution)/shard_map/all_to_all | solution.py:80
  75.5 20.4 %all_gather.12 = bf16[32,16,256]{2,1,0:T(8,128)(2,1)} all-gather(bf16[4,16,256]{2,1,0:T(8,128)(2,1)S(1)} %copy.28), channel_id=1, replica_groups=mesh['z'=8,'c'=2,'x'=4,'y'=8] {'y'}, dimensions={0}, use_global_device_ids=true | all-gather | bytes 294912 | tf_op jit(solution)/shard_map/all_gather | solution.py:74
  95.9 8.8 %collective-permute-start.2 = (bf16[512,1344]{0,1:T(8,128)(2,1)}, bf16[512,1344]{0,1:T(8,128)(2,1)}, u32[]{:S(2)}, u32[]{:S(2)}) collective-permute-start(bf16[512,1344]{0,1:T(8,128)(2,1)} %collective-permute-done.1), channel_id=1, source_target_pairs={{0,32},{32,0},{64,96},{96,64},{128,160},{160,128},{192,224},{224,1... | collective-permute-start | bytes 4128776 | tf_op jit(solution)/shard_map/ppermute | solution.py:55
  104.7 1.3 fusion.108
  106.0 2.2 collective-permute-start.5
  108.2 0.3 convolution_add_fusion.4
  108.5 1.4 fusion.41
  110.0 1.5 fusion
  111.4 1.9 collective-permute-start.4
  113.7 0.3 fusion.34
  114.1 1.4 fusion.38
  115.5 9.9 %collective-permute-done.5 = bf16[512,1344]{0,1:T(8,128)(2,1)S(1)} collective-permute-done((bf16[512,1344]{0,1:T(8,128)(2,1)S(1)}, bf16[512,1344]{0,1:T(8,128)(2,1)S(1)}, u32[]{:S(2)}, u32[]{:S(2)}) %collective-permute-start.5) | collective-permute-done | bytes 1376288 | tf_op jit(solution)/shard_map/ppermute | solution.py:49
  125.5 3.4 %collective-permute-start.7 = (bf16[512,1344]{0,1:T(8,128)(2,1)S(1)}, bf16[512,1344]{0,1:T(8,128)(2,1)S(1)}, u32[]{:S(2)}, u32[]{:S(2)}) collective-permute-start(bf16[512,1344]{0,1:T(8,128)(2,1)S(1)} %collective-permute-done.5), channel_id=1, source_target_pairs={{0,64},{64,128},{128,192},{192,256},{256,320},{320,384},{384,448},... | collective-permute-start | bytes 4128776 | tf_op jit(solution)/shard_map/ppermute | solution.py:49
  128.8 1.5 fusion.3
  130.3 2.4 %collective-permute-start.6 = (bf16[512,1344]{0,1:T(8,128)(2,1)S(1)}, bf16[512,1344]{0,1:T(8,128)(2,1)S(1)}, u32[]{:S(2)}, u32[]{:S(2)}) collective-permute-start(bf16[512,1344]{0,1:T(8,128)(2,1)S(1)} %collective-permute-done.5), channel_id=1, source_target_pairs={{0,32},{32,0},{64,96},{96,64},{128,160},{160,128},{192,224},{224,1... | collective-permute-start | bytes 4128776 | tf_op jit(solution)/shard_map/ppermute | solution.py:55
  132.7 0.3 fusion.29
  133.1 0.3 fusion.27
  133.4 0.3 fusion.31
  133.8 0.4 fusion.6
  134.1 10.7 %collective-permute-done.7 = bf16[512,1344]{0,1:T(8,128)(2,1)S(1)} collective-permute-done((bf16[512,1344]{0,1:T(8,128)(2,1)S(1)}, bf16[512,1344]{0,1:T(8,128)(2,1)S(1)}, u32[]{:S(2)}, u32[]{:S(2)}) %collective-permute-start.7) | collective-permute-done | bytes 1376288 | tf_op jit(solution)/shard_map/ppermute | solution.py:49
  145.1 0.3 fusion.20
  145.5 0.3 fusion.24
  145.9 0.4 fusion.9
  146.2 0.5 copy-done.7
  147.0 6.1 %collective-permute-start.8 = (bf16[128,896]{0,1:T(8,128)(2,1)S(1)}, bf16[128,896]{0,1:T(8,128)(2,1)}, u32[]{:S(2)}, u32[]{:S(2)}) collective-permute-start(bf16[128,896]{0,1:T(8,128)(2,1)S(1)} %pad_maximum_fusion.2), channel_id=1, source_target_pairs={{0,32},{32,0},{64,96},{96,64},{128,160},{160,128},{192,224},{224,1... | collective-permute-start | bytes 688136 | tf_op jit(solution)/shard_map/ppermute | solution.py:44
  153.1 1.2 collective-permute-done.8
  154.3 1.8 pad_maximum_fusion.1
  156.0 1.9 collective-permute-start.9
  158.1 0.8 copy.26
  158.9 0.8 copy.31
  160.3 1.8 copy.36
  162.7 1.3 convolution_add_fusion.9
  164.0 1.9 collective-permute-done.9
  165.9 4.3 %collective-permute-start.10 = (bf16[256,896]{0,1:T(8,128)(2,1)}, bf16[256,896]{0,1:T(8,128)(2,1)S(1)}, u32[]{:S(2)}, u32[]{:S(2)}) collective-permute-start(bf16[256,896]{0,1:T(8,128)(2,1)} %collective-permute-done.9), channel_id=1, source_target_pairs={{0,32},{32,0},{64,96},{96,64},{128,160},{160,128},{192,224},{224,1... | collective-permute-start | bytes 1376264 | tf_op jit(solution)/shard_map/ppermute | solution.py:55
  170.2 1.9 collective-permute-start.11
  172.1 1.3 fusion.75
  173.4 1.3 fusion.19
  174.7 5.3 %collective-permute-done.11 = bf16[256,896]{0,1:T(8,128)(2,1)S(1)} collective-permute-done((bf16[256,896]{0,1:T(8,128)(2,1)}, bf16[256,896]{0,1:T(8,128)(2,1)S(1)}, u32[]{:S(2)}, u32[]{:S(2)}) %collective-permute-start.11) | collective-permute-done | bytes 458784 | tf_op jit(solution)/shard_map/ppermute | solution.py:49
  179.9 4.0 %collective-permute-start.12 = (bf16[256,896]{0,1:T(8,128)(2,1)S(1)}, bf16[256,896]{0,1:T(8,128)(2,1)S(1)}, u32[]{:S(2)}, u32[]{:S(2)}) collective-permute-start(bf16[256,896]{0,1:T(8,128)(2,1)S(1)} %collective-permute-done.11), channel_id=1, source_target_pairs={{0,32},{32,0},{64,96},{96,64},{128,160},{160,128},{192,224},{224,1... | collective-permute-start | bytes 1376264 | tf_op jit(solution)/shard_map/ppermute | solution.py:55
  183.9 1.9 collective-permute-start.13
  186.8 0.3 fusion.18
  187.2 6.2 %collective-permute-done.13 = bf16[256,896]{0,1:T(8,128)(2,1)S(1)} collective-permute-done((bf16[256,896]{0,1:T(8,128)(2,1)S(1)}, bf16[256,896]{0,1:T(8,128)(2,1)S(1)}, u32[]{:S(2)}, u32[]{:S(2)}) %collective-permute-start.13) | collective-permute-done | bytes 458784 | tf_op jit(solution)/shard_map/ppermute | solution.py:49
  193.4 4.0 %collective-permute-start.14 = (bf16[256,896]{0,1:T(8,128)(2,1)S(1)}, bf16[256,896]{0,1:T(8,128)(2,1)S(1)}, u32[]{:S(2)}, u32[]{:S(2)}) collective-permute-start(bf16[256,896]{0,1:T(8,128)(2,1)S(1)} %collective-permute-done.13), channel_id=1, source_target_pairs={{0,32},{32,0},{64,96},{96,64},{128,160},{160,128},{192,224},{224,1... | collective-permute-start | bytes 1376264 | tf_op jit(solution)/shard_map/ppermute | solution.py:55
  197.4 2.1 collective-permute-start.15
  200.5 0.4 fusion.15
  201.0 6.0 %collective-permute-done.15 = bf16[256,896]{0,1:T(8,128)(2,1)S(1)} collective-permute-done((bf16[256,896]{0,1:T(8,128)(2,1)S(1)}, bf16[256,896]{0,1:T(8,128)(2,1)S(1)}, u32[]{:S(2)}, u32[]{:S(2)}) %collective-permute-start.15) | collective-permute-done | bytes 458784 | tf_op jit(solution)/shard_map/ppermute | solution.py:49
  207.9 0.4 fusion.12
  208.4 0.5 copy-done.1
  209.0 0.6 subtract_convert_fusion
  209.5 1.0 copy.33
  210.5 1.0 copy.34
  211.4 0.8 copy.32
  (49 shorter events, 5.2 us)
Async XLA Ops:
  7.2 97.5 %all-gather.6.cloned.1.call-start = ((), (), s32[]{:S(2)}) async-start(), calls=%async_computation.2 | async-start | bytes 1310720 | tf_op jit(solution)/shard_map/all_gather | solution.py:75
  10.1 10.5 %collective-permute-start = (bf16[256,1344]{0,1:T(8,128)(2,1)S(1)}, bf16[256,1344]{0,1:T(8,128)(2,1)S(1)}, u32[]{:S(2)}, u32[]{:S(2)}) collective-permute-start(bf16[256,1344]{0,1:T(8,128)(2,1)S(1)} %constant_dynamic-update-slice_fusion), channel_id=1, source_target_pairs={{0,32},{32,0},{64,96},{96,64},{128,160},{160,128},{192,224},{224,1... | collective-permute-start | bytes 2064392 | tf_op jit(solution)/shard_map/ppermute | solution.py:44
  20.7 39.9 %copy-start.8 = (s32[16]{0:T(128)S(1)}, s32[16]{0:T(128)}, u32[]{:S(2)}) copy-start(s32[16]{0:T(128)} %param.15) | copy-start | bytes 196
  20.7 28.2 %collective-permute-start.1 = (bf16[512,1344]{0,1:T(8,128)(2,1)S(1)}, bf16[512,1344]{0,1:T(8,128)(2,1)}, u32[]{:S(2)}, u32[]{:S(2)}) collective-permute-start(bf16[512,1344]{0,1:T(8,128)(2,1)S(1)} %pad_maximum_fusion), channel_id=1, source_target_pairs={{0,64},{64,128},{128,192},{192,256},{256,320},{320,384},{384,448},... | collective-permute-start | bytes 4128776 | tf_op jit(solution)/shard_map/ppermute | solution.py:49
  48.9 57.1 %collective-permute-start.3 = (bf16[512,1344]{0,1:T(8,128)(2,1)}, bf16[512,1344]{0,1:T(8,128)(2,1)S(1)}, u32[]{:S(2)}, u32[]{:S(2)}) collective-permute-start(bf16[512,1344]{0,1:T(8,128)(2,1)} %collective-permute-done.1), channel_id=1, source_target_pairs={{0,64},{64,128},{128,192},{192,256},{256,320},{320,384},{384,448},... | collective-permute-start | bytes 4128776 | tf_op jit(solution)/shard_map/ppermute | solution.py:49
  50.8 24.6 %all-to-all-start = ((bf16[4,16,256]{2,0,1:T(4,128)(2,1)}), bf16[4,16,256]{2,0,1:T(4,128)(2,1)S(1)}, u32[]{:S(2)}, u32[]{:S(2)}) async-start(bf16[4,16,256]{2,0,1:T(4,128)(2,1)} %bitcast), calls=%async_computation | async-start | bytes 65536 | tf_op jit(solution)/shard_map/all_to_all | solution.py:80
  60.3 100.0 %all-gather.4.cloned.1.call-start = ((), (), s32[]{:S(2)}) async-start(), calls=%async_computation.1 | async-start | bytes 1310720 | tf_op jit(solution)/shard_map/all_gather | solution.py:75
  95.9 18.1 %collective-permute-start.2 = (bf16[512,1344]{0,1:T(8,128)(2,1)}, bf16[512,1344]{0,1:T(8,128)(2,1)}, u32[]{:S(2)}, u32[]{:S(2)}) collective-permute-start(bf16[512,1344]{0,1:T(8,128)(2,1)} %collective-permute-done.1), channel_id=1, source_target_pairs={{0,32},{32,0},{64,96},{96,64},{128,160},{160,128},{192,224},{224,1... | collective-permute-start | bytes 4128776 | tf_op jit(solution)/shard_map/ppermute | solution.py:55
  104.7 3.5 %copy-start = (bf16[128,4096]{1,0:T(8,128)(2,1)S(1)}, bf16[128,4096]{1,0:T(8,128)(2,1)}, u32[]{:S(2)}) copy-start(bf16[128,4096]{1,0:T(8,128)(2,1)} %all-gather.6.cloned.1.call-done) | copy-start | bytes 3145732
  106.0 19.5 %collective-permute-start.5 = (bf16[512,1344]{0,1:T(8,128)(2,1)S(1)}, bf16[512,1344]{0,1:T(8,128)(2,1)S(1)}, u32[]{:S(2)}, u32[]{:S(2)}) collective-permute-start(bf16[512,1344]{0,1:T(8,128)(2,1)S(1)} %collective-permute-done.3), channel_id=1, source_target_pairs={{0,64},{64,128},{128,192},{192,256},{256,320},{320,384},{384,448},... | collective-permute-start | bytes 4128776 | tf_op jit(solution)/shard_map/ppermute | solution.py:49
  111.4 22.0 %collective-permute-start.4 = (bf16[512,1344]{0,1:T(8,128)(2,1)S(1)}, bf16[512,1344]{0,1:T(8,128)(2,1)S(1)}, u32[]{:S(2)}, u32[]{:S(2)}) collective-permute-start(bf16[512,1344]{0,1:T(8,128)(2,1)S(1)} %collective-permute-done.3), channel_id=1, source_target_pairs={{0,32},{32,0},{64,96},{96,64},{128,160},{160,128},{192,224},{224,1... | collective-permute-start | bytes 4128776 | tf_op jit(solution)/shard_map/ppermute | solution.py:55
  125.5 19.3 %collective-permute-start.7 = (bf16[512,1344]{0,1:T(8,128)(2,1)S(1)}, bf16[512,1344]{0,1:T(8,128)(2,1)S(1)}, u32[]{:S(2)}, u32[]{:S(2)}) collective-permute-start(bf16[512,1344]{0,1:T(8,128)(2,1)S(1)} %collective-permute-done.5), channel_id=1, source_target_pairs={{0,64},{64,128},{128,192},{192,256},{256,320},{320,384},{384,448},... | collective-permute-start | bytes 4128776 | tf_op jit(solution)/shard_map/ppermute | solution.py:49
  130.3 15.2 %collective-permute-start.6 = (bf16[512,1344]{0,1:T(8,128)(2,1)S(1)}, bf16[512,1344]{0,1:T(8,128)(2,1)S(1)}, u32[]{:S(2)}, u32[]{:S(2)}) collective-permute-start(bf16[512,1344]{0,1:T(8,128)(2,1)S(1)} %collective-permute-done.5), channel_id=1, source_target_pairs={{0,32},{32,0},{64,96},{96,64},{128,160},{160,128},{192,224},{224,1... | collective-permute-start | bytes 4128776 | tf_op jit(solution)/shard_map/ppermute | solution.py:55
  145.9 0.9 copy-start.7
  146.8 11.3 %copy-start.3 = (bf16[256,448]{0,1:T(8,128)(2,1)S(1)}, bf16[256,448]{0,1:T(8,128)(2,1)}, u32[]{:S(2)}) copy-start(bf16[256,448]{0,1:T(8,128)(2,1)} %param.10) | copy-start | bytes 688132
  146.8 12.2 %copy-start.4 = (bf16[256,448]{0,1:T(8,128)(2,1)S(1)}, bf16[256,448]{0,1:T(8,128)(2,1)}, u32[]{:S(2)}) copy-start(bf16[256,448]{0,1:T(8,128)(2,1)} %param.12) | copy-start | bytes 688132
  146.9 12.8 %copy-start.5 = (f32[256,448]{0,1:T(8,128)S(1)}, f32[256,448]{0,1:T(8,128)}, u32[]{:S(2)}) copy-start(f32[256,448]{0,1:T(8,128)} %param.13) | copy-start | bytes 1376260
  147.0 13.0 %copy-start.6 = (f32[256,448]{0,1:T(8,128)S(1)}, f32[256,448]{0,1:T(8,128)}, u32[]{:S(2)}) copy-start(f32[256,448]{0,1:T(8,128)} %param.14) | copy-start | bytes 1376260
  147.0 7.3 %collective-permute-start.8 = (bf16[128,896]{0,1:T(8,128)(2,1)S(1)}, bf16[128,896]{0,1:T(8,128)(2,1)}, u32[]{:S(2)}, u32[]{:S(2)}) collective-permute-start(bf16[128,896]{0,1:T(8,128)(2,1)S(1)} %pad_maximum_fusion.2), channel_id=1, source_target_pairs={{0,32},{32,0},{64,96},{96,64},{128,160},{160,128},{192,224},{224,1... | collective-permute-start | bytes 688136 | tf_op jit(solution)/shard_map/ppermute | solution.py:44
  156.0 9.8 %collective-permute-start.9 = (bf16[256,896]{0,1:T(8,128)(2,1)}, bf16[256,896]{0,1:T(8,128)(2,1)}, u32[]{:S(2)}, u32[]{:S(2)}) collective-permute-start(bf16[256,896]{0,1:T(8,128)(2,1)} %pad_maximum_fusion.1), channel_id=1, source_target_pairs={{0,64},{64,128},{128,192},{192,256},{256,320},{320,384},{384,448},... | collective-permute-start | bytes 1376264 | tf_op jit(solution)/shard_map/ppermute | solution.py:49
  165.9 20.6 %collective-permute-start.10 = (bf16[256,896]{0,1:T(8,128)(2,1)}, bf16[256,896]{0,1:T(8,128)(2,1)S(1)}, u32[]{:S(2)}, u32[]{:S(2)}) collective-permute-start(bf16[256,896]{0,1:T(8,128)(2,1)} %collective-permute-done.9), channel_id=1, source_target_pairs={{0,32},{32,0},{64,96},{96,64},{128,160},{160,128},{192,224},{224,1... | collective-permute-start | bytes 1376264 | tf_op jit(solution)/shard_map/ppermute | solution.py:55
  170.2 9.7 %collective-permute-start.11 = (bf16[256,896]{0,1:T(8,128)(2,1)}, bf16[256,896]{0,1:T(8,128)(2,1)S(1)}, u32[]{:S(2)}, u32[]{:S(2)}) collective-permute-start(bf16[256,896]{0,1:T(8,128)(2,1)} %collective-permute-done.9), channel_id=1, source_target_pairs={{0,64},{64,128},{128,192},{192,256},{256,320},{320,384},{384,448},... | collective-permute-start | bytes 1376264 | tf_op jit(solution)/shard_map/ppermute | solution.py:49
  179.9 20.2 %collective-permute-start.12 = (bf16[256,896]{0,1:T(8,128)(2,1)S(1)}, bf16[256,896]{0,1:T(8,128)(2,1)S(1)}, u32[]{:S(2)}, u32[]{:S(2)}) collective-permute-start(bf16[256,896]{0,1:T(8,128)(2,1)S(1)} %collective-permute-done.11), channel_id=1, source_target_pairs={{0,32},{32,0},{64,96},{96,64},{128,160},{160,128},{192,224},{224,1... | collective-permute-start | bytes 1376264 | tf_op jit(solution)/shard_map/ppermute | solution.py:55
  183.9 9.5 %collective-permute-start.13 = (bf16[256,896]{0,1:T(8,128)(2,1)S(1)}, bf16[256,896]{0,1:T(8,128)(2,1)S(1)}, u32[]{:S(2)}, u32[]{:S(2)}) collective-permute-start(bf16[256,896]{0,1:T(8,128)(2,1)S(1)} %collective-permute-done.11), channel_id=1, source_target_pairs={{0,64},{64,128},{128,192},{192,256},{256,320},{320,384},{384,448},... | collective-permute-start | bytes 1376264 | tf_op jit(solution)/shard_map/ppermute | solution.py:49
  193.4 14.1 %collective-permute-start.14 = (bf16[256,896]{0,1:T(8,128)(2,1)S(1)}, bf16[256,896]{0,1:T(8,128)(2,1)S(1)}, u32[]{:S(2)}, u32[]{:S(2)}) collective-permute-start(bf16[256,896]{0,1:T(8,128)(2,1)S(1)} %collective-permute-done.13), channel_id=1, source_target_pairs={{0,32},{32,0},{64,96},{96,64},{128,160},{160,128},{192,224},{224,1... | collective-permute-start | bytes 1376264 | tf_op jit(solution)/shard_map/ppermute | solution.py:55
  197.4 9.5 %collective-permute-start.15 = (bf16[256,896]{0,1:T(8,128)(2,1)S(1)}, bf16[256,896]{0,1:T(8,128)(2,1)S(1)}, u32[]{:S(2)}, u32[]{:S(2)}) collective-permute-start(bf16[256,896]{0,1:T(8,128)(2,1)S(1)} %collective-permute-done.13), channel_id=1, source_target_pairs={{0,64},{64,128},{128,192},{192,256},{256,320},{320,384},{384,448},... | collective-permute-start | bytes 1376264 | tf_op jit(solution)/shard_map/ppermute | solution.py:49
  207.9 1.0 copy-start.1
  207.9 1.0 copy-start.2
Sparse Core Ops, SparseCore 0:
  49.0 27.4 all-gather.5
  96.0 29.7 all-gather.3

commit v3 on v2

--- a/solution.py
+++ b/solution.py
@@ -2,6 +2,7 @@
 import jax.numpy as jnp
 from jax import lax
 from jax.sharding import PartitionSpec as P
+
 
 first_decay = 0.9
 second_decay = 0.999
@@ -60,7 +61,29 @@
     return pieces
 
 
-def body(
+def ring_gather(a, name):
+    n = lax.axis_size(name)
+    idx = lax.axis_index(name)
+    fwd = [(i, (i + 1) % n) for i in range(n)]
+    bwd = [(i, (i - 1) % n) for i in range(n)]
+    n_f = n // 2
+    n_b = n - 1 - n_f
+    rel = [None] * n
+    rel[0] = a
+    f = a
+    b = a
+    for k in range(1, n_f + 1):
+        f = lax.ppermute(f, name, fwd)
+        rel[n - k] = f
+        if k <= n_b:
+            b = lax.ppermute(b, name, bwd)
+            rel[k] = b
+    stacked = jnp.stack(rel, 0)
+    ordered = jnp.roll(stacked, idx, axis=0)
+    return ordered.reshape((n * a.shape[0],) + a.shape[1:])
+
+
+def step(
     tokens, hidden_grad, gate_weight, up_weight, gate_probe, gate_mean, gate_curve, group_counts
 ):
     n_dp = lax.axis_size(DP)
@@ -70,16 +93,12 @@
     width = gate_weight.shape[1]
     d = lax.axis_index(DP)
 
-    def gather_mp(a):
-        a = lax.all_gather(a, "y", axis=0, tiled=True)
-        return lax.all_gather(a, "x", axis=0, tiled=True)
-
-    whole = gather_mp(tokens)
+    whole = ring_gather(ring_gather(tokens, "y"), "x")
     group_rows = whole.shape[0]
     t3 = tokens.reshape(rows_loc, n_dp, shard)
     a2a = lax.all_to_all(t3, DP, split_axis=1, concat_axis=1, tiled=True)
     cols = (
-        gather_mp(a2a)
+        lax.all_gather(a2a, MP, axis=0, tiled=True)
         .reshape(n_mp, rows_loc, n_dp, shard)
         .transpose(2, 0, 1, 3)
         .reshape(n_dp * group_rows, shard)
@@ -124,7 +143,7 @@
     )
     every = DP + MP
     return jax.shard_map(
-        body,
+        step,
         mesh=mesh4,
         in_specs=(
             P(every, None),

time: 221 us -> 242 us (1.095)
  starting transfers between devices: 70.4 us -> 119 us
  blocking collectives: 42.5 us -> 0 us
  waiting for transfers between devices: 56.7 us -> 76.5 us
  matrix products: 19 us -> 13.5 us
    all_gather x2 -> x0, blocking collectives: 42.5 us -> none  [gather_mp(): a = lax.all_gather(a, 'y', axis=0, tiled=True)]
    ppermute x0 -> x10, starting transfers between devices: none -> 31.2 us  [the longest x4 19.7 us: ring_gather(): b = lax.ppermute(b, name, bwd)]
    ppermute x0 -> x10, waiting for transfers between devices: none -> 20.9 us  [the longest x6 20.9 us: ring_gather(): f = lax.ppermute(f, name, fwd)]
    ppermute x8, waiting for transfers between devices: 40 us -> 54.4 us  [chip_ring(): cur = lax.ppermute(cur, DP, ring)]
    all_to_all x1, waiting for transfers between devices: 13.6 us -> 0.01 us  [step(): a2a = lax.all_to_all(t3, DP, split_axis=1, concat_axis=1, tiled=True)]
    ppermute x6, starting transfers between devices: 25.4 us -> 34.2 us  [chip_ring(): ex = lax.ppermute(cur, DP, partner)]
    ppermute x8, starting transfers between devices: 20.6 us -> 27.3 us  [chip_ring(): cur = lax.ppermute(cur, DP, ring)]
    dot_general x32, matrix products: 19 us -> 13.5 us  [the longest x16 8.05 us: step(): lax.dot_general(part, piece, (((0,), (0,)), ((), ())), preferred_element_...]
  transfers between devices with their start and end apart: 19 -> 28, of which waited for: 9 -> 13; matrix products, arithmetic and copies ran while one was open for 12% -> 10% of each run, Pallas kernels for 0% -> 0%
where the time goes in v3:
time: 242 us; the launch traced here: 241 us
  starting transfers between devices  119 us (49%)
  waiting for transfers between devices  76.5 us (32%)
  between operations  15.3 us (6%)
  local copies, waits for them, and re-layouts  14.6 us (6%)
  matrix products  13.5 us (6%)
    ppermute x8, waiting for transfers between devices, chip_ring(): cur = lax.ppermute(cur, DP, ring)  54.4 us
    ppermute x6, starting transfers between devices, chip_ring(): ex = lax.ppermute(cur, DP, partner)  34.2 us
    ppermute x8, starting transfers between devices, chip_ring(): cur = lax.ppermute(cur, DP, ring)  27.3 us
    ppermute x6, waiting for transfers between devices, ring_gather(): f = lax.ppermute(f, name, fwd)  20.9 us
    ppermute x4, starting transfers between devices, ring_gather(): b = lax.ppermute(b, name, bwd)  19.7 us
    ppermute x2, starting transfers between devices, chip_ring(): px = lax.ppermute(x, DP, partner)  19.3 us
    ppermute x6, starting transfers between devices, ring_gather(): f = lax.ppermute(f, name, fwd)  11.5 us
    unnamed x49, local copies, waits for them, and re-layouts  9.97 us
  transfers between devices with their start and end apart: 28, of which 13 were waited for; matrix products, arithmetic and copies ran while one was open for 10% of the time, Pallas kernels for 0%

profile of v3, /device:TPU:1, one launch (start us, length us, event | category | flops | bytes accessed | tf_op | source)
XLA Modules:
  0.0 240.9 jit_solution(9100640184894712286)
XLA Ops:
  7.2 5.9 %collective-permute-start = (bf16[4,4096]{1,0:T(4,128)(2,1)}, bf16[4,4096]{1,0:T(4,128)(2,1)S(1)}, u32[]{:S(2)}, u32[]{:S(2)}) collective-permute-start(bf16[4,4096]{1,0:T(4,128)(2,1)} %param.8), channel_id=1, source_target_pairs={{0,7},{1,0},{2,1},{3,2},{4,3},{5,4},{6,5},{7,6},{8,15},{9,8},{10,9... | collective-permute-start | bytes 98312 | tf_op jit(solution)/shard_map/ppermute | solution.py:79
  13.1 1.9 collective-permute-start.3
  15.0 1.0 constant_dynamic-update-slice_fusion.20
  16.0 1.0 constant_dynamic-update-slice_fusion.19
  16.9 1.0 constant_dynamic-update-slice_fusion.18
  17.9 6.8 %collective-permute-start.10 = (bf16[256,1344]{0,1:T(8,128)(2,1)S(1)}, bf16[256,1344]{0,1:T(8,128)(2,1)S(1)}, u32[]{:S(2)}, u32[]{:S(2)}) collective-permute-start(bf16[256,1344]{0,1:T(8,128)(2,1)S(1)} %constant_dynamic-update-slice_fusion.18), channel_id=1, source_target_pairs={{0,32},{32,0},{64,96},{96,64},{128,160},{160,128},{192,224},{224,1... | collective-permute-start | bytes 2064392 | tf_op jit(solution)/shard_map/ppermute | solution.py:45
  24.7 6.6 %all-to-all-start = ((bf16[4,16,256]{2,0,1:T(4,128)(2,1)}), bf16[4,16,256]{2,0,1:T(4,128)(2,1)S(1)}, u32[]{:S(2)}, u32[]{:S(2)}) async-start(bf16[4,16,256]{2,0,1:T(4,128)(2,1)} %bitcast), calls=%async_computation | async-start | bytes 65536 | tf_op jit(solution)/shard_map/all_to_all | solution.py:99
  31.3 0.8 constant_dynamic-update-slice_fusion.15
  32.1 0.6 dynamic_slice.109
  32.7 0.6 compare_convert_fusion
  33.6 4.9 %collective-permute-start.1 = (bf16[4,4096]{1,0:T(4,128)(2,1)S(1)}, bf16[4,4096]{1,0:T(4,128)(2,1)S(1)}, u32[]{:S(2)}, u32[]{:S(2)}) collective-permute-start(bf16[4,4096]{1,0:T(4,128)(2,1)S(1)} %collective-permute-done), channel_id=1, source_target_pairs={{0,7},{1,0},{2,1},{3,2},{4,3},{5,4},{6,5},{7,6},{8,15},{9,8},{10,9... | collective-permute-start | bytes 98312 | tf_op jit(solution)/shard_map/ppermute | solution.py:79
  38.5 1.9 collective-permute-start.4
  40.5 0.6 copy.28
  41.1 4.6 %collective-permute-start.2 = (bf16[4,4096]{1,0:T(4,128)(2,1)S(1)}, bf16[4,4096]{1,0:T(4,128)(2,1)S(1)}, u32[]{:S(2)}, u32[]{:S(2)}) collective-permute-start(bf16[4,4096]{1,0:T(4,128)(2,1)S(1)} %collective-permute-done.1), channel_id=1, source_target_pairs={{0,7},{1,0},{2,1},{3,2},{4,3},{5,4},{6,5},{7,6},{8,15},{9,8},{10,9... | collective-permute-start | bytes 98312 | tf_op jit(solution)/shard_map/ppermute | solution.py:79
  45.7 1.9 collective-permute-start.5
  47.7 3.9 %collective-permute-done.5 = bf16[4,4096]{1,0:T(4,128)(2,1)S(1)} collective-permute-done((bf16[4,4096]{1,0:T(4,128)(2,1)S(1)}, bf16[4,4096]{1,0:T(4,128)(2,1)S(1)}, u32[]{:S(2)}, u32[]{:S(2)}) %collective-permute-start.5) | collective-permute-done | bytes 32800 | tf_op jit(solution)/shard_map/ppermute | solution.py:76
  51.6 1.9 collective-permute-start.6
  53.5 3.9 %collective-permute-done.6 = bf16[4,4096]{1,0:T(4,128)(2,1)S(1)} collective-permute-done((bf16[4,4096]{1,0:T(4,128)(2,1)S(1)}, bf16[4,4096]{1,0:T(4,128)(2,1)S(1)}, u32[]{:S(2)}, u32[]{:S(2)}) %collective-permute-start.6) | collective-permute-done | bytes 32800 | tf_op jit(solution)/shard_map/ppermute | solution.py:76
  57.5 0.8 constant_dynamic-update-slice_fusion.7
  58.8 4.4 %collective-permute-start.7 = (bf16[32,4096]{1,0:T(8,128)(2,1)S(1)}, bf16[32,4096]{1,0:T(8,128)(2,1)S(1)}, u32[]{:S(2)}, u32[]{:S(2)}) collective-permute-start(bf16[32,4096]{1,0:T(8,128)(2,1)S(1)} %reshape.29), channel_id=1, source_target_pairs={{0,24},{8,0},{16,8},{24,16},{1,25},{9,1},{17,9},{25,17},{2,26},{10... | collective-permute-start | bytes 786440 | tf_op jit(solution)/shard_map/ppermute | solution.py:79
  63.2 1.9 collective-permute-start.8
  65.1 6.8 %collective-permute-done.8 = bf16[32,4096]{1,0:T(8,128)(2,1)S(1)} collective-permute-done((bf16[32,4096]{1,0:T(8,128)(2,1)S(1)}, bf16[32,4096]{1,0:T(8,128)(2,1)S(1)}, u32[]{:S(2)}, u32[]{:S(2)}) %collective-permute-start.8) | collective-permute-done | bytes 262176 | tf_op jit(solution)/shard_map/ppermute | solution.py:76
  71.9 1.9 collective-permute-start.9
  73.8 6.4 %collective-permute-done.9 = bf16[32,4096]{1,0:T(8,128)(2,1)S(1)} collective-permute-done((bf16[32,4096]{1,0:T(8,128)(2,1)S(1)}, bf16[32,4096]{1,0:T(8,128)(2,1)S(1)}, u32[]{:S(2)}, u32[]{:S(2)}) %collective-permute-start.9) | collective-permute-done | bytes 262176 | tf_op jit(solution)/shard_map/ppermute | solution.py:76
  80.4 4.6 %collective-permute-start.11 = (bf16[512,1344]{0,1:T(8,128)(2,1)S(1)}, bf16[512,1344]{0,1:T(8,128)(2,1)S(1)}, u32[]{:S(2)}, u32[]{:S(2)}) collective-permute-start(bf16[512,1344]{0,1:T(8,128)(2,1)S(1)} %pad_maximum_fusion), channel_id=1, source_target_pairs={{0,64},{64,128},{128,192},{192,256},{256,320},{320,384},{384,448},... | collective-permute-start | bytes 4128776 | tf_op jit(solution)/shard_map/ppermute | solution.py:50
  85.0 15.2 %collective-permute-done.11 = bf16[512,1344]{0,1:T(8,128)(2,1)S(1)} collective-permute-done((bf16[512,1344]{0,1:T(8,128)(2,1)S(1)}, bf16[512,1344]{0,1:T(8,128)(2,1)S(1)}, u32[]{:S(2)}, u32[]{:S(2)}) %collective-permute-start.11) | collective-permute-done | bytes 1376288 | tf_op jit(solution)/shard_map/ppermute | solution.py:50
  100.2 5.0 %collective-permute-start.13 = (bf16[512,1344]{0,1:T(8,128)(2,1)S(1)}, bf16[512,1344]{0,1:T(8,128)(2,1)S(1)}, u32[]{:S(2)}, u32[]{:S(2)}) collective-permute-start(bf16[512,1344]{0,1:T(8,128)(2,1)S(1)} %collective-permute-done.11), channel_id=1, source_target_pairs={{0,64},{64,128},{128,192},{192,256},{256,320},{320,384},{384,448},... | collective-permute-start | bytes 4128776 | tf_op jit(solution)/shard_map/ppermute | solution.py:50
  105.4 6.5 %collective-permute-start.12 = (bf16[512,1344]{0,1:T(8,128)(2,1)S(1)}, bf16[512,1344]{0,1:T(8,128)(2,1)S(1)}, u32[]{:S(2)}, u32[]{:S(2)}) collective-permute-start(bf16[512,1344]{0,1:T(8,128)(2,1)S(1)} %collective-permute-done.11), channel_id=1, source_target_pairs={{0,32},{32,0},{64,96},{96,64},{128,160},{160,128},{192,224},{224,1... | collective-permute-start | bytes 4128776 | tf_op jit(solution)/shard_map/ppermute | solution.py:56
  112.2 8.2 %collective-permute-done.13 = bf16[512,1344]{0,1:T(8,128)(2,1)S(1)} collective-permute-done((bf16[512,1344]{0,1:T(8,128)(2,1)S(1)}, bf16[512,1344]{0,1:T(8,128)(2,1)S(1)}, u32[]{:S(2)}, u32[]{:S(2)}) %collective-permute-start.13) | collective-permute-done | bytes 1376288 | tf_op jit(solution)/shard_map/ppermute | solution.py:50
  120.5 5.0 %collective-permute-start.15 = (bf16[512,1344]{0,1:T(8,128)(2,1)S(1)}, bf16[512,1344]{0,1:T(8,128)(2,1)S(1)}, u32[]{:S(2)}, u32[]{:S(2)}) collective-permute-start(bf16[512,1344]{0,1:T(8,128)(2,1)S(1)} %collective-permute-done.13), channel_id=1, source_target_pairs={{0,64},{64,128},{128,192},{192,256},{256,320},{320,384},{384,448},... | collective-permute-start | bytes 4128776 | tf_op jit(solution)/shard_map/ppermute | solution.py:50
  126.2 0.4 fusion
  126.5 7.0 %collective-permute-start.14 = (bf16[512,1344]{0,1:T(8,128)(2,1)S(1)}, bf16[512,1344]{0,1:T(8,128)(2,1)S(1)}, u32[]{:S(2)}, u32[]{:S(2)}) collective-permute-start(bf16[512,1344]{0,1:T(8,128)(2,1)S(1)} %collective-permute-done.13), channel_id=1, source_target_pairs={{0,32},{32,0},{64,96},{96,64},{128,160},{160,128},{192,224},{224,1... | collective-permute-start | bytes 4128776 | tf_op jit(solution)/shard_map/ppermute | solution.py:56
  134.6 6.1 %collective-permute-done.15 = bf16[512,1344]{0,1:T(8,128)(2,1)S(1)} collective-permute-done((bf16[512,1344]{0,1:T(8,128)(2,1)S(1)}, bf16[512,1344]{0,1:T(8,128)(2,1)S(1)}, u32[]{:S(2)}, u32[]{:S(2)}) %collective-permute-start.15) | collective-permute-done | bytes 1376288 | tf_op jit(solution)/shard_map/ppermute | solution.py:50
  140.7 5.0 %collective-permute-start.17 = (bf16[512,1344]{0,1:T(8,128)(2,1)S(1)}, bf16[512,1344]{0,1:T(8,128)(2,1)S(1)}, u32[]{:S(2)}, u32[]{:S(2)}) collective-permute-start(bf16[512,1344]{0,1:T(8,128)(2,1)S(1)} %collective-permute-done.15), channel_id=1, source_target_pairs={{0,64},{64,128},{128,192},{192,256},{256,320},{320,384},{384,448},... | collective-permute-start | bytes 4128776 | tf_op jit(solution)/shard_map/ppermute | solution.py:50
  145.7 0.4 fusion.3
  146.1 8.2 %collective-permute-start.16 = (bf16[512,1344]{0,1:T(8,128)(2,1)S(1)}, bf16[512,1344]{0,1:T(8,128)(2,1)S(1)}, u32[]{:S(2)}, u32[]{:S(2)}) collective-permute-start(bf16[512,1344]{0,1:T(8,128)(2,1)S(1)} %collective-permute-done.15), channel_id=1, source_target_pairs={{0,32},{32,0},{64,96},{96,64},{128,160},{160,128},{192,224},{224,1... | collective-permute-start | bytes 4128776 | tf_op jit(solution)/shard_map/ppermute | solution.py:56
  155.3 0.4 fusion.6
  155.7 5.3 %collective-permute-done.17 = bf16[512,1344]{0,1:T(8,128)(2,1)S(1)} collective-permute-done((bf16[512,1344]{0,1:T(8,128)(2,1)S(1)}, bf16[512,1344]{0,1:T(8,128)(2,1)S(1)}, u32[]{:S(2)}, u32[]{:S(2)}) %collective-permute-start.17) | collective-permute-done | bytes 1376288 | tf_op jit(solution)/shard_map/ppermute | solution.py:50
  162.4 0.5 copy-done.7
  163.1 12.6 %collective-permute-start.18 = (bf16[128,896]{0,1:T(8,128)(2,1)S(1)}, bf16[128,896]{0,1:T(8,128)(2,1)S(1)}, u32[]{:S(2)}, u32[]{:S(2)}) collective-permute-start(bf16[128,896]{0,1:T(8,128)(2,1)S(1)} %pad_maximum_fusion.2), channel_id=1, source_target_pairs={{0,32},{32,0},{64,96},{96,64},{128,160},{160,128},{192,224},{224,1... | collective-permute-start | bytes 688136 | tf_op jit(solution)/shard_map/ppermute | solution.py:45
  175.7 1.1 collective-permute-done.18
  176.8 0.8 pad_maximum_fusion.1
  177.7 1.9 collective-permute-start.19
  179.7 0.8 copy.26
  180.5 0.8 copy.31
  181.9 1.8 copy.36
  184.3 1.3 convolution_add_fusion.9
  185.6 1.9 collective-permute-done.19
  187.5 4.3 %collective-permute-start.20 = (bf16[256,896]{0,1:T(8,128)(2,1)}, bf16[256,896]{0,1:T(8,128)(2,1)S(1)}, u32[]{:S(2)}, u32[]{:S(2)}) collective-permute-start(bf16[256,896]{0,1:T(8,128)(2,1)} %collective-permute-done.19), channel_id=1, source_target_pairs={{0,32},{32,0},{64,96},{96,64},{128,160},{160,128},{192,224},{224,1... | collective-permute-start | bytes 1376264 | tf_op jit(solution)/shard_map/ppermute | solution.py:56
  191.8 1.9 collective-permute-start.21
  193.7 1.3 fusion.75
  195.0 1.3 fusion.19
  196.3 5.3 %collective-permute-done.21 = bf16[256,896]{0,1:T(8,128)(2,1)S(1)} collective-permute-done((bf16[256,896]{0,1:T(8,128)(2,1)}, bf16[256,896]{0,1:T(8,128)(2,1)S(1)}, u32[]{:S(2)}, u32[]{:S(2)}) %collective-permute-start.21) | collective-permute-done | bytes 458784 | tf_op jit(solution)/shard_map/ppermute | solution.py:50
  201.5 4.0 %collective-permute-start.22 = (bf16[256,896]{0,1:T(8,128)(2,1)S(1)}, bf16[256,896]{0,1:T(8,128)(2,1)S(1)}, u32[]{:S(2)}, u32[]{:S(2)}) collective-permute-start(bf16[256,896]{0,1:T(8,128)(2,1)S(1)} %collective-permute-done.21), channel_id=1, source_target_pairs={{0,32},{32,0},{64,96},{96,64},{128,160},{160,128},{192,224},{224,1... | collective-permute-start | bytes 1376264 | tf_op jit(solution)/shard_map/ppermute | solution.py:56
  205.5 1.9 collective-permute-start.23
  208.8 6.2 %collective-permute-done.23 = bf16[256,896]{0,1:T(8,128)(2,1)S(1)} collective-permute-done((bf16[256,896]{0,1:T(8,128)(2,1)S(1)}, bf16[256,896]{0,1:T(8,128)(2,1)S(1)}, u32[]{:S(2)}, u32[]{:S(2)}) %collective-permute-start.23) | collective-permute-done | bytes 458784 | tf_op jit(solution)/shard_map/ppermute | solution.py:50
  215.0 4.2 %collective-permute-start.24 = (bf16[256,896]{0,1:T(8,128)(2,1)S(1)}, bf16[256,896]{0,1:T(8,128)(2,1)S(1)}, u32[]{:S(2)}, u32[]{:S(2)}) collective-permute-start(bf16[256,896]{0,1:T(8,128)(2,1)S(1)} %collective-permute-done.23), channel_id=1, source_target_pairs={{0,32},{32,0},{64,96},{96,64},{128,160},{160,128},{192,224},{224,1... | collective-permute-start | bytes 1376264 | tf_op jit(solution)/shard_map/ppermute | solution.py:56
  219.2 1.9 collective-permute-start.25
  222.5 6.2 %collective-permute-done.25 = bf16[256,896]{0,1:T(8,128)(2,1)S(1)} collective-permute-done((bf16[256,896]{0,1:T(8,128)(2,1)S(1)}, bf16[256,896]{0,1:T(8,128)(2,1)S(1)}, u32[]{:S(2)}, u32[]{:S(2)}) %collective-permute-start.25) | collective-permute-done | bytes 458784 | tf_op jit(solution)/shard_map/ppermute | solution.py:50
  230.1 0.6 copy-done
  230.7 0.5 subtract_convert_fusion
  231.3 1.0 copy.33
  232.2 1.0 copy.34
  233.2 0.8 copy.32
  (91 shorter events, 10.7 us)
Async XLA Ops:
  7.2 24.9 %copy-start.8 = (s32[16]{0:T(128)S(1)}, s32[16]{0:T(128)}, u32[]{:S(2)}) copy-start(s32[16]{0:T(128)} %param.15) | copy-start | bytes 196
  7.2 26.5 %collective-permute-start = (bf16[4,4096]{1,0:T(4,128)(2,1)}, bf16[4,4096]{1,0:T(4,128)(2,1)S(1)}, u32[]{:S(2)}, u32[]{:S(2)}) collective-permute-start(bf16[4,4096]{1,0:T(4,128)(2,1)} %param.8), channel_id=1, source_target_pairs={{0,7},{1,0},{2,1},{3,2},{4,3},{5,4},{6,5},{7,6},{8,15},{9,8},{10,9... | collective-permute-start | bytes 98312 | tf_op jit(solution)/shard_map/ppermute | solution.py:79
  13.1 25.4 %collective-permute-start.3 = (bf16[4,4096]{1,0:T(4,128)(2,1)}, bf16[4,4096]{1,0:T(4,128)(2,1)S(1)}, u32[]{:S(2)}, u32[]{:S(2)}) collective-permute-start(bf16[4,4096]{1,0:T(4,128)(2,1)} %param.8), channel_id=1, source_target_pairs={{0,1},{1,2},{2,3},{3,4},{4,5},{5,6},{6,7},{7,0},{8,9},{9,10},{10,1... | collective-permute-start | bytes 98312 | tf_op jit(solution)/shard_map/ppermute | solution.py:76
  17.9 62.4 %collective-permute-start.10 = (bf16[256,1344]{0,1:T(8,128)(2,1)S(1)}, bf16[256,1344]{0,1:T(8,128)(2,1)S(1)}, u32[]{:S(2)}, u32[]{:S(2)}) collective-permute-start(bf16[256,1344]{0,1:T(8,128)(2,1)S(1)} %constant_dynamic-update-slice_fusion.18), channel_id=1, source_target_pairs={{0,32},{32,0},{64,96},{96,64},{128,160},{160,128},{192,224},{224,1... | collective-permute-start | bytes 2064392 | tf_op jit(solution)/shard_map/ppermute | solution.py:45
  24.7 15.8 %all-to-all-start = ((bf16[4,16,256]{2,0,1:T(4,128)(2,1)}), bf16[4,16,256]{2,0,1:T(4,128)(2,1)S(1)}, u32[]{:S(2)}, u32[]{:S(2)}) async-start(bf16[4,16,256]{2,0,1:T(4,128)(2,1)} %bitcast), calls=%async_computation | async-start | bytes 65536 | tf_op jit(solution)/shard_map/all_to_all | solution.py:99
  31.2 150.7 %all-gather.2.cloned.1.call-start = ((), (), s32[]{:S(2)}) async-start(), calls=%async_computation.1 | async-start | bytes 1081344 | tf_op jit(solution)/shard_map/all_gather | solution.py:101
  33.6 7.5 %collective-permute-start.1 = (bf16[4,4096]{1,0:T(4,128)(2,1)S(1)}, bf16[4,4096]{1,0:T(4,128)(2,1)S(1)}, u32[]{:S(2)}, u32[]{:S(2)}) collective-permute-start(bf16[4,4096]{1,0:T(4,128)(2,1)S(1)} %collective-permute-done), channel_id=1, source_target_pairs={{0,7},{1,0},{2,1},{3,2},{4,3},{5,4},{6,5},{7,6},{8,15},{9,8},{10,9... | collective-permute-start | bytes 98312 | tf_op jit(solution)/shard_map/ppermute | solution.py:79
  38.5 7.2 %collective-permute-start.4 = (bf16[4,4096]{1,0:T(4,128)(2,1)S(1)}, bf16[4,4096]{1,0:T(4,128)(2,1)S(1)}, u32[]{:S(2)}, u32[]{:S(2)}) collective-permute-start(bf16[4,4096]{1,0:T(4,128)(2,1)S(1)} %collective-permute-done.3), channel_id=1, source_target_pairs={{0,1},{1,2},{2,3},{3,4},{4,5},{5,6},{6,7},{7,0},{8,9},{9,10},{10,1... | collective-permute-start | bytes 98312 | tf_op jit(solution)/shard_map/ppermute | solution.py:76
  41.1 12.4 %collective-permute-start.2 = (bf16[4,4096]{1,0:T(4,128)(2,1)S(1)}, bf16[4,4096]{1,0:T(4,128)(2,1)S(1)}, u32[]{:S(2)}, u32[]{:S(2)}) collective-permute-start(bf16[4,4096]{1,0:T(4,128)(2,1)S(1)} %collective-permute-done.1), channel_id=1, source_target_pairs={{0,7},{1,0},{2,1},{3,2},{4,3},{5,4},{6,5},{7,6},{8,15},{9,8},{10,9... | collective-permute-start | bytes 98312 | tf_op jit(solution)/shard_map/ppermute | solution.py:79
  45.7 5.9 %collective-permute-start.5 = (bf16[4,4096]{1,0:T(4,128)(2,1)S(1)}, bf16[4,4096]{1,0:T(4,128)(2,1)S(1)}, u32[]{:S(2)}, u32[]{:S(2)}) collective-permute-start(bf16[4,4096]{1,0:T(4,128)(2,1)S(1)} %collective-permute-done.4), channel_id=1, source_target_pairs={{0,1},{1,2},{2,3},{3,4},{4,5},{5,6},{6,7},{7,0},{8,9},{9,10},{10,1... | collective-permute-start | bytes 98312 | tf_op jit(solution)/shard_map/ppermute | solution.py:76
  51.6 5.9 %collective-permute-start.6 = (bf16[4,4096]{1,0:T(4,128)(2,1)S(1)}, bf16[4,4096]{1,0:T(4,128)(2,1)S(1)}, u32[]{:S(2)}, u32[]{:S(2)}) collective-permute-start(bf16[4,4096]{1,0:T(4,128)(2,1)S(1)} %collective-permute-done.5), channel_id=1, source_target_pairs={{0,1},{1,2},{2,3},{3,4},{4,5},{5,6},{6,7},{7,0},{8,9},{9,10},{10,1... | collective-permute-start | bytes 98312 | tf_op jit(solution)/shard_map/ppermute | solution.py:76
  58.8 15.0 %collective-permute-start.7 = (bf16[32,4096]{1,0:T(8,128)(2,1)S(1)}, bf16[32,4096]{1,0:T(8,128)(2,1)S(1)}, u32[]{:S(2)}, u32[]{:S(2)}) collective-permute-start(bf16[32,4096]{1,0:T(8,128)(2,1)S(1)} %reshape.29), channel_id=1, source_target_pairs={{0,24},{8,0},{16,8},{24,16},{1,25},{9,1},{17,9},{25,17},{2,26},{10... | collective-permute-start | bytes 786440 | tf_op jit(solution)/shard_map/ppermute | solution.py:79
  63.2 8.7 %collective-permute-start.8 = (bf16[32,4096]{1,0:T(8,128)(2,1)S(1)}, bf16[32,4096]{1,0:T(8,128)(2,1)S(1)}, u32[]{:S(2)}, u32[]{:S(2)}) collective-permute-start(bf16[32,4096]{1,0:T(8,128)(2,1)S(1)} %reshape.29), channel_id=1, source_target_pairs={{0,8},{8,16},{16,24},{24,0},{1,9},{9,17},{17,25},{25,1},{2,10},{10... | collective-permute-start | bytes 786440 | tf_op jit(solution)/shard_map/ppermute | solution.py:76
  71.9 8.3 %collective-permute-start.9 = (bf16[32,4096]{1,0:T(8,128)(2,1)S(1)}, bf16[32,4096]{1,0:T(8,128)(2,1)S(1)}, u32[]{:S(2)}, u32[]{:S(2)}) collective-permute-start(bf16[32,4096]{1,0:T(8,128)(2,1)S(1)} %collective-permute-done.8), channel_id=1, source_target_pairs={{0,8},{8,16},{16,24},{24,0},{1,9},{9,17},{17,25},{25,1},{2,10},{10... | collective-permute-start | bytes 786440 | tf_op jit(solution)/shard_map/ppermute | solution.py:76
  80.4 19.8 %collective-permute-start.11 = (bf16[512,1344]{0,1:T(8,128)(2,1)S(1)}, bf16[512,1344]{0,1:T(8,128)(2,1)S(1)}, u32[]{:S(2)}, u32[]{:S(2)}) collective-permute-start(bf16[512,1344]{0,1:T(8,128)(2,1)S(1)} %pad_maximum_fusion), channel_id=1, source_target_pairs={{0,64},{64,128},{128,192},{192,256},{256,320},{320,384},{384,448},... | collective-permute-start | bytes 4128776 | tf_op jit(solution)/shard_map/ppermute | solution.py:50
  100.2 20.3 %collective-permute-start.13 = (bf16[512,1344]{0,1:T(8,128)(2,1)S(1)}, bf16[512,1344]{0,1:T(8,128)(2,1)S(1)}, u32[]{:S(2)}, u32[]{:S(2)}) collective-permute-start(bf16[512,1344]{0,1:T(8,128)(2,1)S(1)} %collective-permute-done.11), channel_id=1, source_target_pairs={{0,64},{64,128},{128,192},{192,256},{256,320},{320,384},{384,448},... | collective-permute-start | bytes 4128776 | tf_op jit(solution)/shard_map/ppermute | solution.py:50
  105.4 28.9 %collective-permute-start.12 = (bf16[512,1344]{0,1:T(8,128)(2,1)S(1)}, bf16[512,1344]{0,1:T(8,128)(2,1)S(1)}, u32[]{:S(2)}, u32[]{:S(2)}) collective-permute-start(bf16[512,1344]{0,1:T(8,128)(2,1)S(1)} %collective-permute-done.11), channel_id=1, source_target_pairs={{0,32},{32,0},{64,96},{96,64},{128,160},{160,128},{192,224},{224,1... | collective-permute-start | bytes 4128776 | tf_op jit(solution)/shard_map/ppermute | solution.py:56
  120.5 20.3 %collective-permute-start.15 = (bf16[512,1344]{0,1:T(8,128)(2,1)S(1)}, bf16[512,1344]{0,1:T(8,128)(2,1)S(1)}, u32[]{:S(2)}, u32[]{:S(2)}) collective-permute-start(bf16[512,1344]{0,1:T(8,128)(2,1)S(1)} %collective-permute-done.13), channel_id=1, source_target_pairs={{0,64},{64,128},{128,192},{192,256},{256,320},{320,384},{384,448},... | collective-permute-start | bytes 4128776 | tf_op jit(solution)/shard_map/ppermute | solution.py:50
  126.5 28.4 %collective-permute-start.14 = (bf16[512,1344]{0,1:T(8,128)(2,1)S(1)}, bf16[512,1344]{0,1:T(8,128)(2,1)S(1)}, u32[]{:S(2)}, u32[]{:S(2)}) collective-permute-start(bf16[512,1344]{0,1:T(8,128)(2,1)S(1)} %collective-permute-done.13), channel_id=1, source_target_pairs={{0,32},{32,0},{64,96},{96,64},{128,160},{160,128},{192,224},{224,1... | collective-permute-start | bytes 4128776 | tf_op jit(solution)/shard_map/ppermute | solution.py:56
  140.7 20.3 %collective-permute-start.17 = (bf16[512,1344]{0,1:T(8,128)(2,1)S(1)}, bf16[512,1344]{0,1:T(8,128)(2,1)S(1)}, u32[]{:S(2)}, u32[]{:S(2)}) collective-permute-start(bf16[512,1344]{0,1:T(8,128)(2,1)S(1)} %collective-permute-done.15), channel_id=1, source_target_pairs={{0,64},{64,128},{128,192},{192,256},{256,320},{320,384},{384,448},... | collective-permute-start | bytes 4128776 | tf_op jit(solution)/shard_map/ppermute | solution.py:50
  146.1 15.6 %collective-permute-start.16 = (bf16[512,1344]{0,1:T(8,128)(2,1)S(1)}, bf16[512,1344]{0,1:T(8,128)(2,1)S(1)}, u32[]{:S(2)}, u32[]{:S(2)}) collective-permute-start(bf16[512,1344]{0,1:T(8,128)(2,1)S(1)} %collective-permute-done.15), channel_id=1, source_target_pairs={{0,32},{32,0},{64,96},{96,64},{128,160},{160,128},{192,224},{224,1... | collective-permute-start | bytes 4128776 | tf_op jit(solution)/shard_map/ppermute | solution.py:56
  162.0 0.9 copy-start.7
  162.9 16.8 %copy-start.3 = (bf16[256,448]{0,1:T(8,128)(2,1)S(1)}, bf16[256,448]{0,1:T(8,128)(2,1)}, u32[]{:S(2)}) copy-start(bf16[256,448]{0,1:T(8,128)(2,1)} %param.10) | copy-start | bytes 688132
  162.9 17.6 %copy-start.4 = (bf16[256,448]{0,1:T(8,128)(2,1)S(1)}, bf16[256,448]{0,1:T(8,128)(2,1)}, u32[]{:S(2)}) copy-start(bf16[256,448]{0,1:T(8,128)(2,1)} %param.12) | copy-start | bytes 688132
  163.1 18.3 %copy-start.5 = (f32[256,448]{0,1:T(8,128)S(1)}, f32[256,448]{0,1:T(8,128)}, u32[]{:S(2)}) copy-start(f32[256,448]{0,1:T(8,128)} %param.13) | copy-start | bytes 1376260
  163.1 18.5 %copy-start.6 = (f32[256,448]{0,1:T(8,128)S(1)}, f32[256,448]{0,1:T(8,128)}, u32[]{:S(2)}) copy-start(f32[256,448]{0,1:T(8,128)} %param.14) | copy-start | bytes 1376260
  163.1 13.7 %collective-permute-start.18 = (bf16[128,896]{0,1:T(8,128)(2,1)S(1)}, bf16[128,896]{0,1:T(8,128)(2,1)S(1)}, u32[]{:S(2)}, u32[]{:S(2)}) collective-permute-start(bf16[128,896]{0,1:T(8,128)(2,1)S(1)} %pad_maximum_fusion.2), channel_id=1, source_target_pairs={{0,32},{32,0},{64,96},{96,64},{128,160},{160,128},{192,224},{224,1... | collective-permute-start | bytes 688136 | tf_op jit(solution)/shard_map/ppermute | solution.py:45
  176.8 3.7 %copy-start.2 = (bf16[128,896]{0,1:T(8,128)(2,1)}, bf16[128,896]{0,1:T(8,128)(2,1)S(1)}, u32[]{:S(2)}) copy-start(bf16[128,896]{0,1:T(8,128)(2,1)S(1)} %collective-permute-done.18) | copy-start | bytes 688132
  177.7 9.8 %collective-permute-start.19 = (bf16[256,896]{0,1:T(8,128)(2,1)}, bf16[256,896]{0,1:T(8,128)(2,1)}, u32[]{:S(2)}, u32[]{:S(2)}) collective-permute-start(bf16[256,896]{0,1:T(8,128)(2,1)} %pad_maximum_fusion.1), channel_id=1, source_target_pairs={{0,64},{64,128},{128,192},{192,256},{256,320},{320,384},{384,448},... | collective-permute-start | bytes 1376264 | tf_op jit(solution)/shard_map/ppermute | solution.py:50
  187.5 20.6 %collective-permute-start.20 = (bf16[256,896]{0,1:T(8,128)(2,1)}, bf16[256,896]{0,1:T(8,128)(2,1)S(1)}, u32[]{:S(2)}, u32[]{:S(2)}) collective-permute-start(bf16[256,896]{0,1:T(8,128)(2,1)} %collective-permute-done.19), channel_id=1, source_target_pairs={{0,32},{32,0},{64,96},{96,64},{128,160},{160,128},{192,224},{224,1... | collective-permute-start | bytes 1376264 | tf_op jit(solution)/shard_map/ppermute | solution.py:56
  191.8 9.7 %collective-permute-start.21 = (bf16[256,896]{0,1:T(8,128)(2,1)}, bf16[256,896]{0,1:T(8,128)(2,1)S(1)}, u32[]{:S(2)}, u32[]{:S(2)}) collective-permute-start(bf16[256,896]{0,1:T(8,128)(2,1)} %collective-permute-done.19), channel_id=1, source_target_pairs={{0,64},{64,128},{128,192},{192,256},{256,320},{320,384},{384,448},... | collective-permute-start | bytes 1376264 | tf_op jit(solution)/shard_map/ppermute | solution.py:50
  201.5 20.2 %collective-permute-start.22 = (bf16[256,896]{0,1:T(8,128)(2,1)S(1)}, bf16[256,896]{0,1:T(8,128)(2,1)S(1)}, u32[]{:S(2)}, u32[]{:S(2)}) collective-permute-start(bf16[256,896]{0,1:T(8,128)(2,1)S(1)} %collective-permute-done.21), channel_id=1, source_target_pairs={{0,32},{32,0},{64,96},{96,64},{128,160},{160,128},{192,224},{224,1... | collective-permute-start | bytes 1376264 | tf_op jit(solution)/shard_map/ppermute | solution.py:56
  205.5 9.5 %collective-permute-start.23 = (bf16[256,896]{0,1:T(8,128)(2,1)S(1)}, bf16[256,896]{0,1:T(8,128)(2,1)S(1)}, u32[]{:S(2)}, u32[]{:S(2)}) collective-permute-start(bf16[256,896]{0,1:T(8,128)(2,1)S(1)} %collective-permute-done.21), channel_id=1, source_target_pairs={{0,64},{64,128},{128,192},{192,256},{256,320},{320,384},{384,448},... | collective-permute-start | bytes 1376264 | tf_op jit(solution)/shard_map/ppermute | solution.py:50
  215.0 14.3 %collective-permute-start.24 = (bf16[256,896]{0,1:T(8,128)(2,1)S(1)}, bf16[256,896]{0,1:T(8,128)(2,1)S(1)}, u32[]{:S(2)}, u32[]{:S(2)}) collective-permute-start(bf16[256,896]{0,1:T(8,128)(2,1)S(1)} %collective-permute-done.23), channel_id=1, source_target_pairs={{0,32},{32,0},{64,96},{96,64},{128,160},{160,128},{192,224},{224,1... | collective-permute-start | bytes 1376264 | tf_op jit(solution)/shard_map/ppermute | solution.py:56
  219.2 9.5 %collective-permute-start.25 = (bf16[256,896]{0,1:T(8,128)(2,1)S(1)}, bf16[256,896]{0,1:T(8,128)(2,1)S(1)}, u32[]{:S(2)}, u32[]{:S(2)}) collective-permute-start(bf16[256,896]{0,1:T(8,128)(2,1)S(1)} %collective-permute-done.23), channel_id=1, source_target_pairs={{0,64},{64,128},{128,192},{192,256},{256,320},{320,384},{384,448},... | collective-permute-start | bytes 1376264 | tf_op jit(solution)/shard_map/ppermute | solution.py:50
  229.7 1.0 copy-start
  229.7 1.0 copy-start.1
Sparse Core Ops, SparseCore 0:
  41.2 75.8 all-gather.1
